TPU v7x, 32 devices: a whole 2x2x4 slice. The times are simulated.
32 devices in a mesh: pool: 8 (over z, x), col: 4 (over y, core).
Axes of the slice: x: 2, y: 2, z: 4, core: 2. Of those that a mesh axis runs over, the one named last changes fastest.
Arguments:
- elements: float32 [8, 128, 2048], P('pool', None, 'col'), may hold values from -6 to 6
- index_map: int32 [8, 2048], P('pool', 'col'), may hold values from 0 to 2047, as said below
- band_energy: float32 [8], P('pool'), may hold values from 0.5 to 3
- eval_energy: float32 [2], replicated, may hold values from -1 to 1
- pole_strength: float32 [2048, 2048], P(None, 'col'), may hold values from -0.0078125 to 0.0078125
- pole_frequency: float32 [2048, 2048], P(None, 'col'), may hold values from 0.5 to 4
Outputs:
- sigma: float32 [2, 128, 128], replicated
Inputs may be any that keep to these rules, and one draw needn't show every extreme that they name: For every band, the entries of index_map in columns c * 512 to (c + 1) * 512 - 1 are those same indices in some order, for every column group c.
All inputs are finite; a program needn't handle non-finite values.
Results may differ from a plain program's by a relative error of at most 0.0003.
Values sent between devices are 32-bit elements; how exact they have to be, the bound alone decides.
No kernel may reach another device: no remote copies, remote signals or barrier semaphores. Data moves between devices by JAX's collectives and lax.ppermute only.
A program may use at most 64 MiB of HBM per device.

v0:
```python
import jax
import jax.numpy as jnp
from jax import lax
from jax.sharding import PartitionSpec as P

broadening = 0.5


def mix_rows(band_rows, pole_weight, pole_frequency, eval_energy, band_level):
    highest = lax.Precision.HIGHEST
    results = []
    for energy in range(eval_energy.shape[0]):
        offset = eval_energy[energy] - band_level - pole_frequency
        tile_now = pole_weight * offset / (offset * offset + broadening * broadening)
        results.append(
            jnp.dot(band_rows, tile_now, precision=highest, preferred_element_type=jnp.float32)
        )
    return jnp.concatenate(results, axis=1)


def permute_band(band_rows, band_index_row):
    highest = lax.Precision.HIGHEST
    columns = band_rows.shape[-1]
    source = lax.broadcasted_iota(jnp.int32, (columns, columns), 0)
    selector = (band_index_row[None, :] == source).astype(jnp.float32)
    return jnp.dot(band_rows, selector, precision=highest, preferred_element_type=jnp.float32)


def local(elements, index_map, band_energy, eval_energy, pole_strength, pole_frequency):
    highest = lax.Precision.HIGHEST
    states = elements.shape[1]
    columns = elements.shape[2]
    energies = eval_energy.shape[0]
    column_group = lax.axis_index("col")
    local_index = index_map - column_group * columns
    ordered = jnp.stack([permute_band(elements[0], local_index[0])])
    pole_weight = pole_strength / (2.0 * pole_frequency)
    mixed_list = mix_rows(
        lax.all_gather(ordered[0], "col", axis=1, tiled=True),
        pole_weight,
        pole_frequency,
        eval_energy,
        band_energy[0],
    )
    shaped = mixed_list.reshape(states, energies, columns)
    local_sigma = jnp.einsum("mej,nj->emn", shaped, ordered[0], precision=highest)
    result = lax.psum(local_sigma, ("pool", "col"))
    return result


def solution(mesh):
    placed = (
        P("pool", None, "col"),
        P("pool", "col"),
        P("pool"),
        P(),
        P(None, "col"),
        P(None, "col"),
    )
    return jax.shard_map(local, mesh=mesh, in_specs=placed, out_specs=P(), check_vma=False)
```

profile of v0, /device:TPU:0, one launch (start us, length us, event | category | flops | bytes accessed | tf_op | source)
XLA Modules:
  0.0 174.7 jit_solution(7117824040149415541)
XLA Ops:
  6.5 0.0 copy-start
  6.5 0.0 all-gather.2.cloned.1.call-start
  6.5 0.7 broadcast_subtract_fusion
  7.3 0.2 copy-done
  7.5 1.4 fusion.9
  8.9 0.0 all-gather.2.cloned.1.call-update
  8.9 0.0 all-reduce.2.cloned.1.call-start
  9.6 1.3 fusion.20
  12.2 16.3 %all-gather.2.cloned.1.call-done = f32[128,2048]{0,1:T(8,128)} async-done(((f32[128,512]{0,1:T(8,128)}), f32[128,2048]{0,1:T(8,128)}) %all-gather.2.cloned.1.call-update) | async-done | bytes 1048592 | tf_op jit(solution)/shard_map/all_gather | solution.py:39
  28.5 0.0 copy-start.2
  28.5 0.0 copy-start.3
  28.5 0.0 copy-start.4
  28.5 7.7 %fusion.1 = f32[128,512]{1,0:T(8,128)S(1)} fusion(f32[128,2048]{0,1:T(8,128)} %all-gather.2.cloned.1.call-done, f32[2048,512]{1,0:T(8,128)} %param.11, f32[2048,512]{1,0:T(8,128)} %param.10, f32[]{:T(128)} %bitcast.5), kind=kOutput, calls=%fused_computation.4 | convolution fusion | flops 1617952768 | bytes 9699332 | tf_op jit(solution)/shard_map/dot_general | solution.py:16
  36.2 0.0 copy-done.2
  36.3 0.0 copy-done.3
  36.3 0.0 copy-done.4
  36.3 0.0 copy-start.1
  36.3 3.9 %fusion = f32[128,512]{1,0:T(8,128)S(1)} fusion(f32[128,2048]{0,1:T(8,128)S(1)} %copy-done.4, f32[2048,512]{1,0:T(8,128)S(1)} %copy-done.2, f32[2048,512]{1,0:T(8,128)S(1)} %copy-done.3, f32[]{:T(128)} %bitcast.4), kind=kOutput, calls=%fused_computation.3 | convolution fusion | flops 1617952768 | bytes 9699332 | tf_op jit(solution)/shard_map/dot_general | solution.py:16
  40.3 0.0 copy-done.1
  40.3 1.3 convolution_bitcast_fusion
  41.5 0.0 all-reduce.2.cloned.1.call-update
  41.6 124.6 %all-reduce.2.cloned.1.call-done = f32[2,128,128]{1,2,0:T(8,128)} async-done(((f32[2,128,128]{1,2,0:T(8,128)}), f32[2,128,128]{1,2,0:T(8,128)}) %all-reduce.2.cloned.1.call-update) | async-done | bytes 131088 | tf_op jit(solution)/shard_map/psum | solution.py:47
  166.2 1.7 copy.9
  (1 shorter events, 0.0 us)
Async XLA Ops:
  6.5 1.0 copy-start
  6.5 22.0 %all-gather.2.cloned.1.call-start = ((), (), s32[]{:S(2)}) async-start(), calls=%async_computation | async-start | bytes 1310720 | tf_op jit(solution)/shard_map/all_gather | solution.py:39
  8.9 157.2 %all-reduce.2.cloned.1.call-start = ((), (), s32[]{:S(2)}) async-start(), calls=%async_computation.1 | async-start | bytes 262144 | tf_op jit(solution)/shard_map/psum | solution.py:47
  28.5 7.7 %copy-start.2 = (f32[2048,512]{1,0:T(8,128)S(1)}, f32[2048,512]{1,0:T(8,128)}, u32[]{:S(2)}) copy-start(f32[2048,512]{1,0:T(8,128)} %param.11) | copy-start | bytes 12582916
  28.5 7.7 %copy-start.3 = (f32[2048,512]{1,0:T(8,128)S(1)}, f32[2048,512]{1,0:T(8,128)}, u32[]{:S(2)}) copy-start(f32[2048,512]{1,0:T(8,128)} %param.10) | copy-start | bytes 12582916
  28.5 7.7 %copy-start.4 = (f32[128,2048]{0,1:T(8,128)S(1)}, f32[128,2048]{0,1:T(8,128)}, u32[]{:S(2)}) copy-start(f32[128,2048]{0,1:T(8,128)} %all-gather.2.cloned.1.call-done) | copy-start | bytes 3145732
  36.3 4.0 %copy-start.1 = (f32[512,128]{1,0:T(8,128)S(1)}, f32[512,128]{1,0:T(8,128)}, u32[]{:S(2)}) copy-start(f32[512,128]{1,0:T(8,128)} %fusion.9) | copy-start | bytes 786436
Sparse Core Ops, SparseCore 0:
  9.1 19.4 all-gather.1
  41.7 124.4 all-reduce.1
where the time goes:
time: 175 us
  waiting for transfers between devices  141 us (81%)
  between operations  15.4 us (9%)
  matrix products  14.3 us (8%)
  local copies, waits for them, and re-layouts  3.24 us (2%)
    psum x1, waiting for transfers between devices, local(): result = lax.psum(local_sigma, ('pool', 'col'))  125 us
    all_gather x1, waiting for transfers between devices, local(): lax.all_gather(ordered[0], 'col', axis=1, tiled=True)  16.3 us
    dot_general x2, matrix products, mix_rows(): jnp.dot(band_rows, tile_now, precision=highest, preferred_element_type=jn...  11.6 us
  transfers between devices with their start and end apart: 2, of which 2 were waited for; matrix products, arithmetic and copies ran while one was open for 1% of the time, Pallas kernels for 0%

commit v1 on v0

v1 whole, which is shorter than its diff:
```python
import jax
import jax.numpy as jnp
from jax import lax
from jax.sharding import PartitionSpec as P

broadening = 0.5


def permute_band(band_rows, band_index_row):
    highest = lax.Precision.HIGHEST
    columns = band_rows.shape[-1]
    source = lax.broadcasted_iota(jnp.int32, (columns, columns), 0)
    selector = (band_index_row[None, :] == source).astype(jnp.float32)
    return jnp.dot(band_rows, selector, precision=highest, preferred_element_type=jnp.float32)


def is_power_of_two(n):
    return n > 0 and (n & (n - 1)) == 0


def exchange(value, axis, size, partner):
    return lax.ppermute(value, axis, [(i, partner(i)) for i in range(size)])


def butterfly_sum(value, axes, size):
    stage = 1
    while stage < size:
        value = value + exchange(value, axes, size, lambda i, s=stage: i ^ s)
        stage *= 2
    return value


def make_local(col_size, total_size):
    def local(elements, index_map, band_energy, eval_energy, pole_strength, pole_frequency):
        highest = lax.Precision.HIGHEST
        columns = elements.shape[2]
        energies = eval_energy.shape[0]
        column_group = lax.axis_index("col")
        local_index = index_map - column_group * columns
        ordered = permute_band(elements[0], local_index[0])

        if is_power_of_two(col_size):
            sources = [(0, column_group)] + [
                (m, column_group ^ m) for m in range(1, col_size)
            ]
            partner = lambda m: (lambda i: i ^ m)
        else:
            sources = [(0, column_group)] + [
                (m, (column_group + col_size - m) % col_size) for m in range(1, col_size)
            ]
            partner = lambda m: (lambda i: (i + m) % col_size)
        blocks = {0: ordered}
        for m, _ in sources[1:]:
            blocks[m] = exchange(ordered, "col", col_size, partner(m))

        pole_weight = pole_strength / (2.0 * pole_frequency)
        band_level = band_energy[0]
        sigmas = []
        for energy in range(energies):
            mixed = None
            for m, owner in sources:
                start = owner * columns
                weight_rows = lax.dynamic_slice_in_dim(pole_weight, start, columns, axis=0)
                frequency_rows = lax.dynamic_slice_in_dim(pole_frequency, start, columns, axis=0)
                offset = eval_energy[energy] - band_level - frequency_rows
                tile_now = weight_rows * offset / (offset * offset + broadening * broadening)
                part = jnp.dot(blocks[m], tile_now, precision=highest, preferred_element_type=jnp.float32)
                mixed = part if mixed is None else mixed + part
            sigmas.append(
                jnp.dot(mixed, ordered.T, precision=highest, preferred_element_type=jnp.float32)
            )
        local_sigma = jnp.stack(sigmas)
        if is_power_of_two(total_size):
            return butterfly_sum(local_sigma, ("pool", "col"), total_size)
        return lax.psum(local_sigma, ("pool", "col"))

    return local


def solution(mesh):
    placed = (
        P("pool", None, "col"),
        P("pool", "col"),
        P("pool"),
        P(),
        P(None, "col"),
        P(None, "col"),
    )
    col_size = mesh.shape["col"]
    total_size = mesh.shape["pool"] * col_size
    return jax.shard_map(
        make_local(col_size, total_size), mesh=mesh, in_specs=placed, out_specs=P(), check_vma=False
    )
```

time: 175 us -> 50.7 us (0.29)
  waiting for transfers between devices: 141 us -> 16.4 us
  between operations: 15.4 us -> 2.1 us
  starting transfers between devices: 0.04 us -> 11.6 us
  other arithmetic: 0.76 us -> 6.15 us
  matrix products: 14.3 us -> 12.3 us
    psum x1 -> x0, waiting for transfers between devices: 125 us -> none  [local(): result = lax.psum(local_sigma, ('pool', 'col'))]
    ppermute x0 -> x8, waiting for transfers between devices: none -> 16.4 us  [exchange(): return lax.ppermute(value, axis, [(i, partner(i)) for i in range(size)])]
    all_gather x1 -> x0, waiting for transfers between devices: 16.3 us -> none  [local(): lax.all_gather(ordered[0], 'col', axis=1, tiled=True)]
    ppermute x0 -> x8, starting transfers between devices: none -> 11.6 us  [exchange(): return lax.ppermute(value, axis, [(i, partner(i)) for i in range(size)])]
    div x0 -> x1, other arithmetic: none -> 4.66 us  [local(): pole_weight = pole_strength / (2.0 * pole_frequency)]
    dot_general x3 -> x10, matrix products: 12.9 us -> 11.6 us  [the longest x8 10.8 us: local(): jnp.dot(blocks[m], tile_now, precision=highest, preferred_element_type=jn...]
  transfers between devices with their start and end apart: 2 -> 8, of which waited for: 2 -> 5; matrix products, arithmetic and copies ran while one was open for 1% -> 26% of each run, Pallas kernels for 0% -> 0%
where the time goes in v1:
time: 50.7 us; the launch traced here: 50.5 us
  waiting for transfers between devices  16.4 us (32%)
  matrix products  12.3 us (24%)
  starting transfers between devices  11.6 us (23%)
  other arithmetic  6.15 us (12%)
  between operations  2.1 us (4%)
  local copies, waits for them, and re-layouts  1.97 us (4%)
    ppermute x8, waiting for transfers between devices, exchange(): return lax.ppermute(value, axis, [(i, partner(i)) for i in range(size)])  16.4 us
    ppermute x8, starting transfers between devices, exchange(): return lax.ppermute(value, axis, [(i, partner(i)) for i in range(size)])  11.6 us
    dot_general x8, matrix products, local(): jnp.dot(blocks[m], tile_now, precision=highest, preferred_element_type=jn...  10.8 us
    div x1, other arithmetic, local(): pole_weight = pole_strength / (2.0 * pole_frequency)  4.66 us
    slice x1, local copies, waits for them, and re-layouts, local(): offset = eval_energy[energy] - band_level - frequency_rows  1.32 us
  transfers between devices with their start and end apart: 8, of which 5 were waited for; matrix products, arithmetic and copies ran while one was open for 26% of the time, Pallas kernels for 0%

profile of v1, /device:TPU:0, one launch (start us, length us, event | category | flops | bytes accessed | tf_op | source)
XLA Modules:
  0.0 50.5 jit_solution(9793157263793407316)
XLA Ops:
  0.0 0.7 %broadcast_subtract_fusion = s32[1,512]{1,0:T(1,128)S(1)} fusion(s32[1,512]{1,0:T(1,128)} %param.7, s32[]{:T(128)S(6)} %mul.71), kind=kLoop, calls=%fused_computation.79 | loop fusion | flops 512 | bytes 4100 | tf_op jit(solution)/shard_map/sub | solution.py:39
  1.0 0.7 %fusion.35 = f32[512,128]{1,0:T(8,128)S(1)} fusion(s32[512]{0:T(512)S(1)} %bitcast.26, f32[1,128,512]{2,1,0:T(8,128)S(1)} %copy-done), kind=kOutput, calls=%fused_computation.51 | convolution fusion | flops 403177472 | bytes 526336 | tf_op jit(solution)/shard_map/dot_general | solution.py:14
  1.7 2.5 %collective-permute-start.2 = (f32[128,512]{0,1:T(8,128)S(1)}, f32[128,512]{0,1:T(8,128)S(1)}, u32[]{:S(2)}, u32[]{:S(2)}) collective-permute-start(f32[128,512]{0,1:T(8,128)S(1)} %bitcast.23), channel_id=1, source_target_pairs={{0,3},{1,2},{2,1},{3,0},{4,7},{5,6},{6,5},{7,4},{8,11},{9,10},{10,... | collective-permute-start | bytes 786440 | tf_op jit(solution)/shard_map/ppermute | solution.py:22
  4.2 0.6 %collective-permute-start.1 = (f32[128,512]{0,1:T(8,128)S(1)}, f32[128,512]{0,1:T(8,128)S(1)}, u32[]{:S(2)}, u32[]{:S(2)}) collective-permute-start(f32[128,512]{0,1:T(8,128)S(1)} %bitcast.24), channel_id=1, source_target_pairs={{0,2},{1,3},{2,0},{3,1},{4,6},{5,7},{6,4},{7,5},{8,10},{9,11},{10,... | collective-permute-start | bytes 786440 | tf_op jit(solution)/shard_map/ppermute | solution.py:22
  5.5 1.3 %fusion.72 = (f32[1]{0:T(128)}, f32[1]{0:T(128)}) fusion(f32[2]{0:T(128)} %param.9), kind=kLoop, calls=%fused_computation.89 | loop fusion | bytes 16 | tf_op jit(solution)/shard_map/slice | solution.py:65
  7.4 4.7 %multiply_divide_fusion = f32[2048,512]{1,0:T(8,128)S(1)} fusion(f32[2048,512]{1,0:T(8,128)} %param.10, f32[2048,512]{1,0:T(8,128)} %param.11), kind=kLoop, calls=%fused_computation | loop fusion | flops 2097152 | bytes 12582912 | tf_op jit(solution)/shard_map/div | solution.py:56
  12.1 1.0 %fusion.16 = f32[128,512]{1,0:T(8,128)S(1)} fusion(f32[512,128]{1,0:T(8,128)S(1)} %fusion.35, f32[2048,512]{1,0:T(8,128)S(1)} %copy-done.1, s32[]{:T(128)S(6)} %select_n.8, f32[2048,512]{1,0:T(8,128)S(1)} %multiply_divide_fusion, f32[]{:T(128)} %bitcast.5), kind=kOutput, calls=%fused_computation.32 | convolution fusion | flops 403963904 | bytes 2621448 | tf_op jit(solution)/shard_map/dot_general | solution.py:67
  14.0 1.0 %fusion.14 = f32[128,512]{1,0:T(8,128)S(1)} fusion(f32[512,128]{1,0:T(8,128)S(1)} %fusion.35, f32[2048,512]{1,0:T(8,128)S(1)} %copy-done.1, s32[]{:T(128)S(6)} %select_n.8, f32[2048,512]{1,0:T(8,128)S(1)} %multiply_divide_fusion, f32[]{:T(128)} %bitcast.2), kind=kOutput, calls=%fused_computation.30 | convolution fusion | flops 403963904 | bytes 2621448 | tf_op jit(solution)/shard_map/dot_general | solution.py:67
  15.0 2.6 %fusion.17 = f32[128,512]{1,0:T(8,128)S(1)} fusion(f32[128,512]{0,1:T(8,128)S(1)} %collective-permute-done.2, f32[2048,512]{1,0:T(8,128)} %param.11, s32[]{:T(128)S(6)} %select_n.11, f32[2048,512]{1,0:T(8,128)} %copy-done.3, f32[]{:T(128)} %bitcast.5), kind=kOutput, calls=%fused_computation.33 | convolution fusion | flops 403963904 | bytes 2621956 | tf_op jit(solution)/shard_map/dot_general | solution.py:67
  17.8 2.4 %convolution_add_fusion.1 = f32[128,512]{1,0:T(8,128)S(1)} fusion(f32[128,512]{1,0:T(8,128)S(1)} %fusion.16, f32[128,512]{0,1:T(8,128)S(1)} %collective-permute-done, f32[2048,512]{1,0:T(8,128)S(1)} %copy-done.2, s32[]{:T(128)S(6)} %select_n.9, f32[2048,512]{1,0:T(8,128)} %copy-done.3, f32[]{:T(128)} %bitcast.5), kind=kOutput, calls=%fused_computation.3 | convolution fusion | flops 404029440 | bytes 2884100 | tf_op jit(solution)/shard_map/dot_general | solution.py:67
  20.3 1.0 %fusion = f32[128,512]{1,0:T(8,128)S(1)} fusion(f32[128,512]{1,0:T(8,128)S(1)} %fusion.17, f32[128,512]{1,0:T(8,128)S(1)} %convolution_add_fusion.1, f32[128,512]{0,1:T(8,128)S(1)} %collective-permute-done.1, f32[2048,512]{1,0:T(8,128)S(1)} %copy-done.2, s32[]{:T(128)S(6)} %select_n.10, f32[2048,512]{1,0:T(8,128)S(1)} %copy-done.4, f32[]{:T(128)} %bitcast.5), kind=kOutput, calls=%fused_computation.2 | convolution fusion | flops 404094976 | bytes 3145736 | tf_op jit(solution)/shard_map/dot_general | solution.py:67
  21.7 1.0 %fusion.15 = f32[128,512]{1,0:T(8,128)S(1)} fusion(f32[128,512]{0,1:T(8,128)S(1)} %collective-permute-done.2, f32[2048,512]{1,0:T(8,128)S(1)} %copy-done.2, s32[]{:T(128)S(6)} %select_n.11, f32[2048,512]{1,0:T(8,128)S(1)} %copy-done.4, f32[]{:T(128)} %bitcast.2), kind=kOutput, calls=%fused_computation.31 | convolution fusion | flops 403963904 | bytes 2621448 | tf_op jit(solution)/shard_map/dot_general | solution.py:67
  22.6 1.0 %convolution_add_fusion.3 = f32[128,512]{1,0:T(8,128)S(1)} fusion(f32[128,512]{1,0:T(8,128)S(1)} %fusion.14, f32[128,512]{0,1:T(8,128)S(1)} %collective-permute-done, f32[2048,512]{1,0:T(8,128)S(1)} %copy-done.2, s32[]{:T(128)S(6)} %select_n.9, f32[2048,512]{1,0:T(8,128)S(1)} %copy-done.4, f32[]{:T(128)} %bitcast.2), kind=kOutput, calls=%fused_computation.6 | convolution fusion | flops 404029440 | bytes 2883592 | tf_op jit(solution)/shard_map/dot_general | solution.py:67
  23.6 1.0 %fusion.1 = f32[128,512]{1,0:T(8,128)S(1)} fusion(f32[128,512]{1,0:T(8,128)S(1)} %fusion.15, f32[128,512]{1,0:T(8,128)S(1)} %convolution_add_fusion.3, f32[128,512]{0,1:T(8,128)S(1)} %collective-permute-done.1, f32[2048,512]{1,0:T(8,128)S(1)} %copy-done.2, s32[]{:T(128)S(6)} %select_n.10, f32[2048,512]{1,0:T(8,128)S(1)} %copy-done.4, f32[]{:T(128)} %bitcast.2), kind=kOutput, calls=%fused_computation.5 | convolution fusion | flops 404094976 | bytes 3145736 | tf_op jit(solution)/shard_map/dot_general | solution.py:67
  25.5 1.0 %collective-permute-done.3 = f32[2,128,128]{2,1,0:T(8,128)S(1)} collective-permute-done((f32[2,128,128]{2,1,0:T(8,128)S(1)}, f32[2,128,128]{2,1,0:T(8,128)S(1)}, u32[]{:S(2)}, u32[]{:S(2)}) %collective-permute-start.3) | collective-permute-done | bytes 131104 | tf_op jit(solution)/shard_map/ppermute | solution.py:22
  26.5 1.7 %collective-permute-start.4 = (f32[2,128,128]{2,1,0:T(8,128)S(1)}, f32[2,128,128]{2,1,0:T(8,128)S(1)}, u32[]{:S(2)}, u32[]{:S(2)}) collective-permute-start(f32[2,128,128]{2,1,0:T(8,128)S(1)} %fusion.71), channel_id=1, source_target_pairs={{0,2},{1,3},{2,0},{3,1},{4,6},{5,7},{6,4},{7,5},{8,10},{9,11},{10,... | collective-permute-start | bytes 393224 | tf_op jit(solution)/shard_map/ppermute | solution.py:22
  28.2 4.1 %collective-permute-done.4 = f32[2,128,128]{2,1,0:T(8,128)S(1)} collective-permute-done((f32[2,128,128]{2,1,0:T(8,128)S(1)}, f32[2,128,128]{2,1,0:T(8,128)S(1)}, u32[]{:S(2)}, u32[]{:S(2)}) %collective-permute-start.4) | collective-permute-done | bytes 131104 | tf_op jit(solution)/shard_map/ppermute | solution.py:22
  32.4 1.6 %collective-permute-start.5 = (f32[2,128,128]{2,1,0:T(8,128)S(1)}, f32[2,128,128]{2,1,0:T(8,128)S(1)}, u32[]{:S(2)}, u32[]{:S(2)}) collective-permute-start(f32[2,128,128]{2,1,0:T(8,128)S(1)} %fusion.85), channel_id=1, source_target_pairs={{0,4},{1,5},{2,6},{3,7},{4,0},{5,1},{6,2},{7,3},{8,12},{9,13},{10,... | collective-permute-start | bytes 393224 | tf_op jit(solution)/shard_map/ppermute | solution.py:22
  33.9 3.5 %collective-permute-done.5 = f32[2,128,128]{2,1,0:T(8,128)S(1)} collective-permute-done((f32[2,128,128]{2,1,0:T(8,128)S(1)}, f32[2,128,128]{2,1,0:T(8,128)S(1)}, u32[]{:S(2)}, u32[]{:S(2)}) %collective-permute-start.5) | collective-permute-done | bytes 131104 | tf_op jit(solution)/shard_map/ppermute | solution.py:22
  37.4 1.6 %collective-permute-start.6 = (f32[2,128,128]{2,1,0:T(8,128)S(1)}, f32[2,128,128]{2,1,0:T(8,128)S(1)}, u32[]{:S(2)}, u32[]{:S(2)}) collective-permute-start(f32[2,128,128]{2,1,0:T(8,128)S(1)} %add.101), channel_id=1, source_target_pairs={{0,8},{1,9},{2,10},{3,11},{4,12},{5,13},{6,14},{7,15},{8,0},{9,1},... | collective-permute-start | bytes 393224 | tf_op jit(solution)/shard_map/ppermute | solution.py:22
  39.1 3.4 %collective-permute-done.6 = f32[2,128,128]{2,1,0:T(8,128)S(1)} collective-permute-done((f32[2,128,128]{2,1,0:T(8,128)S(1)}, f32[2,128,128]{2,1,0:T(8,128)S(1)}, u32[]{:S(2)}, u32[]{:S(2)}) %collective-permute-start.6) | collective-permute-done | bytes 131104 | tf_op jit(solution)/shard_map/ppermute | solution.py:22
  42.5 3.0 %collective-permute-start.7 = (f32[2,128,128]{2,1,0:T(8,128)S(1)}, f32[2,128,128]{2,1,0:T(8,128)S(1)}, u32[]{:S(2)}, u32[]{:S(2)}) collective-permute-start(f32[2,128,128]{2,1,0:T(8,128)S(1)} %add.102), channel_id=1, source_target_pairs={{0,16},{1,17},{2,18},{3,19},{4,20},{5,21},{6,22},{7,23},{8,24},{9,... | collective-permute-start | bytes 393224 | tf_op jit(solution)/shard_map/ppermute | solution.py:22
  45.5 4.4 %collective-permute-done.7 = f32[2,128,128]{2,1,0:T(8,128)S(1)} collective-permute-done((f32[2,128,128]{2,1,0:T(8,128)S(1)}, f32[2,128,128]{2,1,0:T(8,128)S(1)}, u32[]{:S(2)}, u32[]{:S(2)}) %collective-permute-start.7) | collective-permute-done | bytes 131104 | tf_op jit(solution)/shard_map/ppermute | solution.py:22
  49.8 0.7 %add.103 = f32[2,128,128]{2,1,0:T(8,128)} add(f32[2,128,128]{2,1,0:T(8,128)S(1)} %add.102, f32[2,128,128]{2,1,0:T(8,128)S(1)} %collective-permute-done.7) | non-fusion elementwise | flops 32768 | bytes 393216 | tf_op jit(solution)/shard_map/add | solution.py:28
  (22 shorter events, 2.1 us)
Async XLA Ops:
  0.0 1.0 %copy-start = (f32[1,128,512]{2,1,0:T(8,128)S(1)}, f32[1,128,512]{2,1,0:T(8,128)}, u32[]{:S(2)}) copy-start(f32[1,128,512]{2,1,0:T(8,128)} %param.6) | copy-start | bytes 786436
  1.7 13.4 %collective-permute-start.2 = (f32[128,512]{0,1:T(8,128)S(1)}, f32[128,512]{0,1:T(8,128)S(1)}, u32[]{:S(2)}, u32[]{:S(2)}) collective-permute-start(f32[128,512]{0,1:T(8,128)S(1)} %bitcast.23), channel_id=1, source_target_pairs={{0,3},{1,2},{2,1},{3,0},{4,7},{5,6},{6,5},{7,4},{8,11},{9,10},{10,... | collective-permute-start | bytes 786440 | tf_op jit(solution)/shard_map/ppermute | solution.py:22
  4.2 16.1 %collective-permute-start.1 = (f32[128,512]{0,1:T(8,128)S(1)}, f32[128,512]{0,1:T(8,128)S(1)}, u32[]{:S(2)}, u32[]{:S(2)}) collective-permute-start(f32[128,512]{0,1:T(8,128)S(1)} %bitcast.24), channel_id=1, source_target_pairs={{0,2},{1,3},{2,0},{3,1},{4,6},{5,7},{6,4},{7,5},{8,10},{9,11},{10,... | collective-permute-start | bytes 786440 | tf_op jit(solution)/shard_map/ppermute | solution.py:22
  4.8 12.9 %collective-permute-start = (f32[128,512]{0,1:T(8,128)S(1)}, f32[128,512]{0,1:T(8,128)S(1)}, u32[]{:S(2)}, u32[]{:S(2)}) collective-permute-start(f32[128,512]{0,1:T(8,128)S(1)} %bitcast.25), channel_id=1, source_target_pairs={{0,1},{1,0},{2,3},{3,2},{4,5},{5,4},{6,7},{7,6},{8,9},{9,8},{10,11... | collective-permute-start | bytes 786440 | tf_op jit(solution)/shard_map/ppermute | solution.py:22
  7.4 4.7 %copy-start.1 = (f32[2048,512]{1,0:T(8,128)S(1)}, f32[2048,512]{1,0:T(8,128)}, u32[]{:S(2)}) copy-start(f32[2048,512]{1,0:T(8,128)} %param.11) | copy-start | bytes 12582916
  12.1 1.9 %copy-start.3 = (f32[2048,512]{1,0:T(8,128)}, f32[2048,512]{1,0:T(8,128)S(1)}, u32[]{:S(2)}) copy-start(f32[2048,512]{1,0:T(8,128)S(1)} %multiply_divide_fusion) | copy-start | bytes 12582916
  15.0 2.8 %copy-start.2 = (f32[2048,512]{1,0:T(8,128)S(1)}, f32[2048,512]{1,0:T(8,128)}, u32[]{:S(2)}) copy-start(f32[2048,512]{1,0:T(8,128)} %param.11) | copy-start | bytes 12582916
  15.0 5.3 %copy-start.4 = (f32[2048,512]{1,0:T(8,128)S(1)}, f32[2048,512]{1,0:T(8,128)}, u32[]{:S(2)}) copy-start(f32[2048,512]{1,0:T(8,128)} %copy-done.3) | copy-start | bytes 12582916
  25.0 1.5 %collective-permute-start.3 = (f32[2,128,128]{2,1,0:T(8,128)S(1)}, f32[2,128,128]{2,1,0:T(8,128)S(1)}, u32[]{:S(2)}, u32[]{:S(2)}) collective-permute-start(f32[2,128,128]{2,1,0:T(8,128)S(1)} %pad_maximum_fusion), channel_id=1, source_target_pairs={{0,1},{1,0},{2,3},{3,2},{4,5},{5,4},{6,7},{7,6},{8,9},{9,8},{10,11... | collective-permute-start | bytes 393224 | tf_op jit(solution)/shard_map/ppermute | solution.py:22
  26.5 5.8 %collective-permute-start.4 = (f32[2,128,128]{2,1,0:T(8,128)S(1)}, f32[2,128,128]{2,1,0:T(8,128)S(1)}, u32[]{:S(2)}, u32[]{:S(2)}) collective-permute-start(f32[2,128,128]{2,1,0:T(8,128)S(1)} %fusion.71), channel_id=1, source_target_pairs={{0,2},{1,3},{2,0},{3,1},{4,6},{5,7},{6,4},{7,5},{8,10},{9,11},{10,... | collective-permute-start | bytes 393224 | tf_op jit(solution)/shard_map/ppermute | solution.py:22
  32.4 5.0 %collective-permute-start.5 = (f32[2,128,128]{2,1,0:T(8,128)S(1)}, f32[2,128,128]{2,1,0:T(8,128)S(1)}, u32[]{:S(2)}, u32[]{:S(2)}) collective-permute-start(f32[2,128,128]{2,1,0:T(8,128)S(1)} %fusion.85), channel_id=1, source_target_pairs={{0,4},{1,5},{2,6},{3,7},{4,0},{5,1},{6,2},{7,3},{8,12},{9,13},{10,... | collective-permute-start | bytes 393224 | tf_op jit(solution)/shard_map/ppermute | solution.py:22
  37.4 5.0 %collective-permute-start.6 = (f32[2,128,128]{2,1,0:T(8,128)S(1)}, f32[2,128,128]{2,1,0:T(8,128)S(1)}, u32[]{:S(2)}, u32[]{:S(2)}) collective-permute-start(f32[2,128,128]{2,1,0:T(8,128)S(1)} %add.101), channel_id=1, source_target_pairs={{0,8},{1,9},{2,10},{3,11},{4,12},{5,13},{6,14},{7,15},{8,0},{9,1},... | collective-permute-start | bytes 393224 | tf_op jit(solution)/shard_map/ppermute | solution.py:22
  42.5 7.3 %collective-permute-start.7 = (f32[2,128,128]{2,1,0:T(8,128)S(1)}, f32[2,128,128]{2,1,0:T(8,128)S(1)}, u32[]{:S(2)}, u32[]{:S(2)}) collective-permute-start(f32[2,128,128]{2,1,0:T(8,128)S(1)} %add.102), channel_id=1, source_target_pairs={{0,16},{1,17},{2,18},{3,19},{4,20},{5,21},{6,22},{7,23},{8,24},{9,... | collective-permute-start | bytes 393224 | tf_op jit(solution)/shard_map/ppermute | solution.py:22

commit v2 on v1

--- a/solution.py
+++ b/solution.py
@@ -53,26 +53,26 @@
         for m, _ in sources[1:]:
             blocks[m] = exchange(ordered, "col", col_size, partner(m))
 
-        pole_weight = pole_strength / (2.0 * pole_frequency)
         band_level = band_energy[0]
         sigmas = []
         for energy in range(energies):
             mixed = None
             for m, owner in sources:
                 start = owner * columns
-                weight_rows = lax.dynamic_slice_in_dim(pole_weight, start, columns, axis=0)
+                strength_rows = lax.dynamic_slice_in_dim(pole_strength, start, columns, axis=0)
                 frequency_rows = lax.dynamic_slice_in_dim(pole_frequency, start, columns, axis=0)
                 offset = eval_energy[energy] - band_level - frequency_rows
-                tile_now = weight_rows * offset / (offset * offset + broadening * broadening)
+                denominator = 2.0 * frequency_rows * (offset * offset + broadening * broadening)
+                tile_now = strength_rows * offset / denominator
                 part = jnp.dot(blocks[m], tile_now, precision=highest, preferred_element_type=jnp.float32)
                 mixed = part if mixed is None else mixed + part
-            sigmas.append(
-                jnp.dot(mixed, ordered.T, precision=highest, preferred_element_type=jnp.float32)
-            )
-        local_sigma = jnp.stack(sigmas)
-        if is_power_of_two(total_size):
-            return butterfly_sum(local_sigma, ("pool", "col"), total_size)
-        return lax.psum(local_sigma, ("pool", "col"))
+            sigma = jnp.dot(mixed, ordered.T, precision=highest, preferred_element_type=jnp.float32)
+            if is_power_of_two(total_size):
+                sigma = butterfly_sum(sigma, ("pool", "col"), total_size)
+            else:
+                sigma = lax.psum(sigma, ("pool", "col"))
+            sigmas.append(sigma)
+        return jnp.stack(sigmas)
 
     return local
 

time: 50.7 us -> 45.4 us (0.90)
  waiting for transfers between devices: 16.4 us -> 7.56 us
  starting transfers between devices: 11.6 us -> 18.2 us
  other arithmetic: 6.15 us -> 1.48 us
  matrix products: 12.3 us -> 14.2 us
    ppermute x8 -> x13, waiting for transfers between devices: 16.4 us -> 7.56 us  [exchange(): return lax.ppermute(value, axis, [(i, partner(i)) for i in range(size)])]
    ppermute x8 -> x13, starting transfers between devices: 11.6 us -> 18.2 us  [exchange(): return lax.ppermute(value, axis, [(i, partner(i)) for i in range(size)])]
    div x1 -> x0, other arithmetic: 4.66 us -> none  [local(): pole_weight = pole_strength / (2.0 * pole_frequency)]
    dot_general x8, matrix products: 10.8 us -> 12.7 us  [local(): jnp.dot(blocks[m], tile_now, precision=highest, preferred_element_type=jn...]
    add x5 -> x8, other arithmetic: 0.75 us -> 0.07 us  [butterfly_sum(): value = value + exchange(value, axes, size, lambda i, s=stage: i ^ s)]
    another operation x1 -> x3, other arithmetic: 0.01 us -> 0.68 us  [local(): return jnp.stack(sigmas)]
  transfers between devices with their start and end apart: 8 -> 13, of which waited for: 5 -> 6; matrix products, arithmetic and copies ran while one was open for 26% -> 30% of each run, Pallas kernels for 0% -> 0%
where the time goes in v2:
time: 45.4 us; the launch traced here: 45.2 us
  starting transfers between devices  18.2 us (40%)
  matrix products  14.2 us (31%)
  waiting for transfers between devices  7.56 us (17%)
  between operations  2.13 us (5%)
  local copies, waits for them, and re-layouts  1.68 us (4%)
  other arithmetic  1.48 us (3%)
    ppermute x13, starting transfers between devices, exchange(): return lax.ppermute(value, axis, [(i, partner(i)) for i in range(size)])  18.2 us
    dot_general x8, matrix products, local(): jnp.dot(blocks[m], tile_now, precision=highest, preferred_element_type=jn...  12.7 us
    ppermute x13, waiting for transfers between devices, exchange(): return lax.ppermute(value, axis, [(i, partner(i)) for i in range(size)])  7.56 us
    slice x1, local copies, waits for them, and re-layouts, local(): offset = eval_energy[energy] - band_level - frequency_rows  1.33 us
  transfers between devices with their start and end apart: 13, of which 6 were waited for; matrix products, arithmetic and copies ran while one was open for 30% of the time, Pallas kernels for 0%

profile of v2, /device:TPU:0, one launch (start us, length us, event | category | flops | bytes accessed | tf_op | source)
XLA Modules:
  0.0 45.2 jit_solution(11489949561335305195)
XLA Ops:
  0.0 0.7 %broadcast_subtract_fusion = s32[1,512]{1,0:T(1,128)S(1)} fusion(s32[1,512]{1,0:T(1,128)} %param.7, s32[]{:T(128)S(6)} %mul.105), kind=kLoop, calls=%fused_computation.98 | loop fusion | flops 512 | bytes 4100 | tf_op jit(solution)/shard_map/sub | solution.py:39
  1.0 0.7 %fusion.47 = f32[512,128]{1,0:T(8,128)S(1)} fusion(s32[512]{0:T(512)S(1)} %bitcast.26, f32[1,128,512]{2,1,0:T(8,128)S(1)} %copy-done), kind=kOutput, calls=%fused_computation.60 | convolution fusion | flops 403177472 | bytes 526336 | tf_op jit(solution)/shard_map/dot_general | solution.py:14
  2.2 2.6 %collective-permute-start.2 = (f32[128,512]{0,1:T(8,128)S(1)}, f32[128,512]{0,1:T(8,128)S(1)}, u32[]{:S(2)}, u32[]{:S(2)}) collective-permute-start(f32[128,512]{0,1:T(8,128)S(1)} %bitcast.24), channel_id=1, source_target_pairs={{0,3},{1,2},{2,1},{3,0},{4,7},{5,6},{6,5},{7,4},{8,11},{9,10},{10,... | collective-permute-start | bytes 786440 | tf_op jit(solution)/shard_map/ppermute | solution.py:22
  4.9 1.3 %fusion.99 = (f32[1]{0:T(128)}, f32[1]{0:T(128)}) fusion(f32[2]{0:T(128)} %param.9), kind=kLoop, calls=%fused_computation.115 | loop fusion | bytes 16 | tf_op jit(solution)/shard_map/slice | solution.py:64
  7.5 2.6 %fusion.18 = f32[128,512]{1,0:T(8,128)S(1)} fusion(f32[512,128]{1,0:T(8,128)S(1)} %fusion.47, f32[2048,512]{1,0:T(8,128)} %param.11, s32[]{:T(128)S(6)} %select_n.8, f32[2048,512]{1,0:T(8,128)} %param.10, f32[]{:T(128)} %bitcast.2), kind=kOutput, calls=%fused_computation.31 | convolution fusion | flops 404488192 | bytes 2621956 | tf_op jit(solution)/shard_map/dot_general | solution.py:67
  10.8 2.7 %fusion.20 = f32[128,512]{1,0:T(8,128)S(1)} fusion(f32[512,128]{1,0:T(8,128)S(1)} %fusion.47, f32[2048,512]{1,0:T(8,128)} %param.11, s32[]{:T(128)S(6)} %select_n.8, f32[2048,512]{1,0:T(8,128)} %param.10, f32[]{:T(128)} %bitcast.5), kind=kOutput, calls=%fused_computation.33 | convolution fusion | flops 404488192 | bytes 2621956 | tf_op jit(solution)/shard_map/dot_general | solution.py:67
  13.6 2.4 %convolution_add_fusion.3 = f32[128,512]{1,0:T(8,128)S(1)} fusion(f32[128,512]{1,0:T(8,128)S(1)} %fusion.18, f32[128,512]{0,1:T(8,128)S(1)} %collective-permute-done, f32[2048,512]{1,0:T(8,128)S(1)} %copy-done.1, s32[]{:T(128)S(6)} %select_n.9, f32[2048,512]{1,0:T(8,128)} %param.10, f32[]{:T(128)} %bitcast.2), kind=kOutput, calls=%fused_computation.5 | convolution fusion | flops 404553728 | bytes 2884100 | tf_op jit(solution)/shard_map/dot_general | solution.py:67
  16.0 1.0 %fusion.19 = f32[128,512]{1,0:T(8,128)S(1)} fusion(f32[128,512]{0,1:T(8,128)S(1)} %collective-permute-done.2, f32[2048,512]{1,0:T(8,128)S(1)} %copy-done.1, s32[]{:T(128)S(6)} %select_n.11, f32[2048,512]{1,0:T(8,128)S(1)} %copy-done.2, f32[]{:T(128)} %bitcast.2), kind=kOutput, calls=%fused_computation.32 | convolution fusion | flops 404488192 | bytes 2621448 | tf_op jit(solution)/shard_map/dot_general | solution.py:67
  17.3 1.0 %fusion.1 = f32[128,512]{1,0:T(8,128)S(1)} fusion(f32[128,512]{1,0:T(8,128)S(1)} %fusion.19, f32[128,512]{1,0:T(8,128)S(1)} %convolution_add_fusion.3, f32[128,512]{0,1:T(8,128)S(1)} %collective-permute-done.1, f32[2048,512]{1,0:T(8,128)S(1)} %copy-done.1, s32[]{:T(128)S(6)} %select_n.10, f32[2048,512]{1,0:T(8,128)S(1)} %copy-done.2, f32[]{:T(128)} %bitcast.2), kind=kOutput, calls=%fused_computation.4 | convolution fusion | flops 404619264 | bytes 3145736 | tf_op jit(solution)/shard_map/dot_general | solution.py:67
  18.8 1.0 %fusion.21 = f32[128,512]{1,0:T(8,128)S(1)} fusion(f32[128,512]{0,1:T(8,128)S(1)} %collective-permute-done.2, f32[2048,512]{1,0:T(8,128)S(1)} %copy-done.1, s32[]{:T(128)S(6)} %select_n.11, f32[2048,512]{1,0:T(8,128)S(1)} %copy-done.2, f32[]{:T(128)} %bitcast.5), kind=kOutput, calls=%fused_computation.34 | convolution fusion | flops 404488192 | bytes 2621448 | tf_op jit(solution)/shard_map/dot_general | solution.py:67
  19.8 1.0 %convolution_add_fusion.1 = f32[128,512]{1,0:T(8,128)S(1)} fusion(f32[128,512]{1,0:T(8,128)S(1)} %fusion.20, f32[128,512]{0,1:T(8,128)S(1)} %collective-permute-done, f32[2048,512]{1,0:T(8,128)S(1)} %copy-done.1, s32[]{:T(128)S(6)} %select_n.9, f32[2048,512]{1,0:T(8,128)S(1)} %copy-done.2, f32[]{:T(128)} %bitcast.5), kind=kOutput, calls=%fused_computation.2 | convolution fusion | flops 404553728 | bytes 2883592 | tf_op jit(solution)/shard_map/dot_general | solution.py:67
  20.9 1.0 %fusion = f32[128,512]{1,0:T(8,128)S(1)} fusion(f32[128,512]{1,0:T(8,128)S(1)} %fusion.21, f32[128,512]{1,0:T(8,128)S(1)} %convolution_add_fusion.1, f32[128,512]{0,1:T(8,128)S(1)} %collective-permute-done.1, f32[2048,512]{1,0:T(8,128)S(1)} %copy-done.1, s32[]{:T(128)S(6)} %select_n.10, f32[2048,512]{1,0:T(8,128)S(1)} %copy-done.2, f32[]{:T(128)} %bitcast.5), kind=kOutput, calls=%fused_computation.1 | convolution fusion | flops 404619264 | bytes 3145736 | tf_op jit(solution)/shard_map/dot_general | solution.py:67
  22.9 1.8 %collective-permute-start.4 = (f32[128,128]{1,0:T(8,128)S(1)}, f32[128,128]{1,0:T(8,128)S(1)}, u32[]{:S(2)}, u32[]{:S(2)}) collective-permute-start(f32[128,128]{1,0:T(8,128)S(1)} %add.107), channel_id=1, source_target_pairs={{0,2},{1,3},{2,0},{3,1},{4,6},{5,7},{6,4},{7,5},{8,10},{9,11},{10,... | collective-permute-start | bytes 196616 | tf_op jit(solution)/shard_map/ppermute | solution.py:22
  24.6 0.9 %collective-permute-start.9 = (f32[128,128]{1,0:T(8,128)S(1)}, f32[128,128]{1,0:T(8,128)S(1)}, u32[]{:S(2)}, u32[]{:S(2)}) collective-permute-start(f32[128,128]{1,0:T(8,128)S(1)} %add.119), channel_id=1, source_target_pairs={{0,2},{1,3},{2,0},{3,1},{4,6},{5,7},{6,4},{7,5},{8,10},{9,11},{10,... | collective-permute-start | bytes 196616 | tf_op jit(solution)/shard_map/ppermute | solution.py:22
  25.5 1.8 %collective-permute-done.4 = f32[128,128]{1,0:T(8,128)S(1)} collective-permute-done((f32[128,128]{1,0:T(8,128)S(1)}, f32[128,128]{1,0:T(8,128)S(1)}, u32[]{:S(2)}, u32[]{:S(2)}) %collective-permute-start.4) | collective-permute-done | bytes 65568 | tf_op jit(solution)/shard_map/ppermute | solution.py:22
  27.3 1.9 %collective-permute-start.5 = (f32[128,128]{1,0:T(8,128)S(1)}, f32[128,128]{1,0:T(8,128)S(1)}, u32[]{:S(2)}, u32[]{:S(2)}) collective-permute-start(f32[128,128]{1,0:T(8,128)S(1)} %add.108), channel_id=1, source_target_pairs={{0,4},{1,5},{2,6},{3,7},{4,0},{5,1},{6,2},{7,3},{8,12},{9,13},{10,... | collective-permute-start | bytes 196616 | tf_op jit(solution)/shard_map/ppermute | solution.py:22
  29.3 1.3 %collective-permute-start.10 = (f32[128,128]{1,0:T(8,128)S(1)}, f32[128,128]{1,0:T(8,128)S(1)}, u32[]{:S(2)}, u32[]{:S(2)}) collective-permute-start(f32[128,128]{1,0:T(8,128)S(1)} %add.120), channel_id=1, source_target_pairs={{0,4},{1,5},{2,6},{3,7},{4,0},{5,1},{6,2},{7,3},{8,12},{9,13},{10,... | collective-permute-start | bytes 196616 | tf_op jit(solution)/shard_map/ppermute | solution.py:22
  30.6 1.2 %collective-permute-done.5 = f32[128,128]{1,0:T(8,128)S(1)} collective-permute-done((f32[128,128]{1,0:T(8,128)S(1)}, f32[128,128]{1,0:T(8,128)S(1)}, u32[]{:S(2)}, u32[]{:S(2)}) %collective-permute-start.5) | collective-permute-done | bytes 65568 | tf_op jit(solution)/shard_map/ppermute | solution.py:22
  31.8 1.9 %collective-permute-start.6 = (f32[128,128]{1,0:T(8,128)S(1)}, f32[128,128]{1,0:T(8,128)S(1)}, u32[]{:S(2)}, u32[]{:S(2)}) collective-permute-start(f32[128,128]{1,0:T(8,128)S(1)} %add.109), channel_id=1, source_target_pairs={{0,8},{1,9},{2,10},{3,11},{4,12},{5,13},{6,14},{7,15},{8,0},{9,1},... | collective-permute-start | bytes 196616 | tf_op jit(solution)/shard_map/ppermute | solution.py:22
  33.7 1.6 %collective-permute-start.11 = (f32[128,128]{1,0:T(8,128)S(1)}, f32[128,128]{1,0:T(8,128)S(1)}, u32[]{:S(2)}, u32[]{:S(2)}) collective-permute-start(f32[128,128]{1,0:T(8,128)S(1)} %add.121), channel_id=1, source_target_pairs={{0,8},{1,9},{2,10},{3,11},{4,12},{5,13},{6,14},{7,15},{8,0},{9,1},... | collective-permute-start | bytes 196616 | tf_op jit(solution)/shard_map/ppermute | solution.py:22
  35.3 0.9 %collective-permute-done.6 = f32[128,128]{1,0:T(8,128)S(1)} collective-permute-done((f32[128,128]{1,0:T(8,128)S(1)}, f32[128,128]{1,0:T(8,128)S(1)}, u32[]{:S(2)}, u32[]{:S(2)}) %collective-permute-start.6) | collective-permute-done | bytes 65568 | tf_op jit(solution)/shard_map/ppermute | solution.py:22
  36.1 3.1 %collective-permute-start.7 = (f32[128,128]{1,0:T(8,128)S(1)}, f32[128,128]{1,0:T(8,128)S(1)}, u32[]{:S(2)}, u32[]{:S(2)}) collective-permute-start(f32[128,128]{1,0:T(8,128)S(1)} %add.110), channel_id=1, source_target_pairs={{0,16},{1,17},{2,18},{3,19},{4,20},{5,21},{6,22},{7,23},{8,24},{9,... | collective-permute-start | bytes 196616 | tf_op jit(solution)/shard_map/ppermute | solution.py:22
  39.3 1.9 %collective-permute-start.12 = (f32[128,128]{1,0:T(8,128)S(1)}, f32[128,128]{1,0:T(8,128)S(1)}, u32[]{:S(2)}, u32[]{:S(2)}) collective-permute-start(f32[128,128]{1,0:T(8,128)S(1)} %add.122), channel_id=1, source_target_pairs={{0,16},{1,17},{2,18},{3,19},{4,20},{5,21},{6,22},{7,23},{8,24},{9,... | collective-permute-start | bytes 196616 | tf_op jit(solution)/shard_map/ppermute | solution.py:22
  41.5 3.0 %collective-permute-done.12 = f32[128,128]{1,0:T(8,128)S(1)} collective-permute-done((f32[128,128]{1,0:T(8,128)S(1)}, f32[128,128]{1,0:T(8,128)S(1)}, u32[]{:S(2)}, u32[]{:S(2)}) %collective-permute-start.12) | collective-permute-done | bytes 65568 | tf_op jit(solution)/shard_map/ppermute | solution.py:22
  (32 shorter events, 3.8 us)
Async XLA Ops:
  0.0 1.0 %copy-start = (f32[1,128,512]{2,1,0:T(8,128)S(1)}, f32[1,128,512]{2,1,0:T(8,128)}, u32[]{:S(2)}) copy-start(f32[1,128,512]{2,1,0:T(8,128)} %param.6) | copy-start | bytes 786436
  1.7 11.8 %collective-permute-start = (f32[128,512]{0,1:T(8,128)S(1)}, f32[128,512]{0,1:T(8,128)S(1)}, u32[]{:S(2)}, u32[]{:S(2)}) collective-permute-start(f32[128,512]{0,1:T(8,128)S(1)} %bitcast.23), channel_id=1, source_target_pairs={{0,1},{1,0},{2,3},{3,2},{4,5},{5,4},{6,7},{7,6},{8,9},{9,8},{10,11... | collective-permute-start | bytes 786440 | tf_op jit(solution)/shard_map/ppermute | solution.py:22
  2.2 13.7 %collective-permute-start.2 = (f32[128,512]{0,1:T(8,128)S(1)}, f32[128,512]{0,1:T(8,128)S(1)}, u32[]{:S(2)}, u32[]{:S(2)}) collective-permute-start(f32[128,512]{0,1:T(8,128)S(1)} %bitcast.24), channel_id=1, source_target_pairs={{0,3},{1,2},{2,1},{3,0},{4,7},{5,6},{6,5},{7,4},{8,11},{9,10},{10,... | collective-permute-start | bytes 786440 | tf_op jit(solution)/shard_map/ppermute | solution.py:22
  4.9 12.5 %collective-permute-start.1 = (f32[128,512]{0,1:T(8,128)S(1)}, f32[128,512]{0,1:T(8,128)S(1)}, u32[]{:S(2)}, u32[]{:S(2)}) collective-permute-start(f32[128,512]{0,1:T(8,128)S(1)} %bitcast.25), channel_id=1, source_target_pairs={{0,2},{1,3},{2,0},{3,1},{4,6},{5,7},{6,4},{7,5},{8,10},{9,11},{10,... | collective-permute-start | bytes 786440 | tf_op jit(solution)/shard_map/ppermute | solution.py:22
  10.8 2.8 %copy-start.1 = (f32[2048,512]{1,0:T(8,128)S(1)}, f32[2048,512]{1,0:T(8,128)}, u32[]{:S(2)}) copy-start(f32[2048,512]{1,0:T(8,128)} %param.11) | copy-start | bytes 12582916
  13.5 2.5 %copy-start.2 = (f32[2048,512]{1,0:T(8,128)S(1)}, f32[2048,512]{1,0:T(8,128)}, u32[]{:S(2)}) copy-start(f32[2048,512]{1,0:T(8,128)} %param.10) | copy-start | bytes 12582916
  18.7 4.1 %collective-permute-start.3 = (f32[128,128]{1,0:T(8,128)S(1)}, f32[128,128]{1,0:T(8,128)S(1)}, u32[]{:S(2)}, u32[]{:S(2)}) collective-permute-start(f32[128,128]{1,0:T(8,128)S(1)} %fusion.100), channel_id=1, source_target_pairs={{0,1},{1,0},{2,3},{3,2},{4,5},{5,4},{6,7},{7,6},{8,9},{9,8},{10,11... | collective-permute-start | bytes 196616 | tf_op jit(solution)/shard_map/ppermute | solution.py:22
  22.3 2.3 %collective-permute-start.8 = (f32[128,128]{1,0:T(8,128)S(1)}, f32[128,128]{1,0:T(8,128)S(1)}, u32[]{:S(2)}, u32[]{:S(2)}) collective-permute-start(f32[128,128]{1,0:T(8,128)S(1)} %fusion.101), channel_id=1, source_target_pairs={{0,1},{1,0},{2,3},{3,2},{4,5},{5,4},{6,7},{7,6},{8,9},{9,8},{10,11... | collective-permute-start | bytes 196616 | tf_op jit(solution)/shard_map/ppermute | solution.py:22
  22.9 4.5 %collective-permute-start.4 = (f32[128,128]{1,0:T(8,128)S(1)}, f32[128,128]{1,0:T(8,128)S(1)}, u32[]{:S(2)}, u32[]{:S(2)}) collective-permute-start(f32[128,128]{1,0:T(8,128)S(1)} %add.107), channel_id=1, source_target_pairs={{0,2},{1,3},{2,0},{3,1},{4,6},{5,7},{6,4},{7,5},{8,10},{9,11},{10,... | collective-permute-start | bytes 196616 | tf_op jit(solution)/shard_map/ppermute | solution.py:22
  24.6 4.6 %collective-permute-start.9 = (f32[128,128]{1,0:T(8,128)S(1)}, f32[128,128]{1,0:T(8,128)S(1)}, u32[]{:S(2)}, u32[]{:S(2)}) collective-permute-start(f32[128,128]{1,0:T(8,128)S(1)} %add.119), channel_id=1, source_target_pairs={{0,2},{1,3},{2,0},{3,1},{4,6},{5,7},{6,4},{7,5},{8,10},{9,11},{10,... | collective-permute-start | bytes 196616 | tf_op jit(solution)/shard_map/ppermute | solution.py:22
  27.3 4.4 %collective-permute-start.5 = (f32[128,128]{1,0:T(8,128)S(1)}, f32[128,128]{1,0:T(8,128)S(1)}, u32[]{:S(2)}, u32[]{:S(2)}) collective-permute-start(f32[128,128]{1,0:T(8,128)S(1)} %add.108), channel_id=1, source_target_pairs={{0,4},{1,5},{2,6},{3,7},{4,0},{5,1},{6,2},{7,3},{8,12},{9,13},{10,... | collective-permute-start | bytes 196616 | tf_op jit(solution)/shard_map/ppermute | solution.py:22
  29.3 4.4 %collective-permute-start.10 = (f32[128,128]{1,0:T(8,128)S(1)}, f32[128,128]{1,0:T(8,128)S(1)}, u32[]{:S(2)}, u32[]{:S(2)}) collective-permute-start(f32[128,128]{1,0:T(8,128)S(1)} %add.120), channel_id=1, source_target_pairs={{0,4},{1,5},{2,6},{3,7},{4,0},{5,1},{6,2},{7,3},{8,12},{9,13},{10,... | collective-permute-start | bytes 196616 | tf_op jit(solution)/shard_map/ppermute | solution.py:22
  31.8 4.3 %collective-permute-start.6 = (f32[128,128]{1,0:T(8,128)S(1)}, f32[128,128]{1,0:T(8,128)S(1)}, u32[]{:S(2)}, u32[]{:S(2)}) collective-permute-start(f32[128,128]{1,0:T(8,128)S(1)} %add.109), channel_id=1, source_target_pairs={{0,8},{1,9},{2,10},{3,11},{4,12},{5,13},{6,14},{7,15},{8,0},{9,1},... | collective-permute-start | bytes 196616 | tf_op jit(solution)/shard_map/ppermute | solution.py:22
  33.7 5.6 %collective-permute-start.11 = (f32[128,128]{1,0:T(8,128)S(1)}, f32[128,128]{1,0:T(8,128)S(1)}, u32[]{:S(2)}, u32[]{:S(2)}) collective-permute-start(f32[128,128]{1,0:T(8,128)S(1)} %add.121), channel_id=1, source_target_pairs={{0,8},{1,9},{2,10},{3,11},{4,12},{5,13},{6,14},{7,15},{8,0},{9,1},... | collective-permute-start | bytes 196616 | tf_op jit(solution)/shard_map/ppermute | solution.py:22
  36.1 5.4 %collective-permute-start.7 = (f32[128,128]{1,0:T(8,128)S(1)}, f32[128,128]{1,0:T(8,128)S(1)}, u32[]{:S(2)}, u32[]{:S(2)}) collective-permute-start(f32[128,128]{1,0:T(8,128)S(1)} %add.110), channel_id=1, source_target_pairs={{0,16},{1,17},{2,18},{3,19},{4,20},{5,21},{6,22},{7,23},{8,24},{9,... | collective-permute-start | bytes 196616 | tf_op jit(solution)/shard_map/ppermute | solution.py:22
  39.3 5.2 %collective-permute-start.12 = (f32[128,128]{1,0:T(8,128)S(1)}, f32[128,128]{1,0:T(8,128)S(1)}, u32[]{:S(2)}, u32[]{:S(2)}) collective-permute-start(f32[128,128]{1,0:T(8,128)S(1)} %add.122), channel_id=1, source_target_pairs={{0,16},{1,17},{2,18},{3,19},{4,20},{5,21},{6,22},{7,23},{8,24},{9,... | collective-permute-start | bytes 196616 | tf_op jit(solution)/shard_map/ppermute | solution.py:22

commit v3 on v2

--- a/solution.py
+++ b/solution.py
@@ -32,7 +32,7 @@
 
 def make_local(col_size, total_size):
     def local(elements, index_map, band_energy, eval_energy, pole_strength, pole_frequency):
-        highest = lax.Precision.HIGHEST
+        high = lax.Precision.HIGH
         columns = elements.shape[2]
         energies = eval_energy.shape[0]
         column_group = lax.axis_index("col")
@@ -64,9 +64,9 @@
                 offset = eval_energy[energy] - band_level - frequency_rows
                 denominator = 2.0 * frequency_rows * (offset * offset + broadening * broadening)
                 tile_now = strength_rows * offset / denominator
-                part = jnp.dot(blocks[m], tile_now, precision=highest, preferred_element_type=jnp.float32)
+                part = jnp.dot(blocks[m], tile_now, precision=high, preferred_element_type=jnp.float32)
                 mixed = part if mixed is None else mixed + part
-            sigma = jnp.dot(mixed, ordered.T, precision=highest, preferred_element_type=jnp.float32)
+            sigma = jnp.dot(mixed, ordered.T, precision=high, preferred_element_type=jnp.float32)
             if is_power_of_two(total_size):
                 sigma = butterfly_sum(sigma, ("pool", "col"), total_size)
             else:

time: 45.4 us -> 43.8 us (0.965)
  matrix products: 14.2 us -> 11.3 us
  waiting for transfers between devices: 7.56 us -> 8.51 us
    dot_general x10, matrix products: 13.5 us -> 10.6 us  [the longest x8 10 us: local(): jnp.dot(blocks[m], tile_now, precision=high, preferred_element_type=jnp.f...]
    ppermute x13, waiting for transfers between devices: 7.56 us -> 8.51 us  [exchange(): return lax.ppermute(value, axis, [(i, partner(i)) for i in range(size)])]
  transfers between devices with their start and end apart: 13 -> 13, of which waited for: 6 -> 6; matrix products, arithmetic and copies ran while one was open for 30% -> 25% of each run, Pallas kernels for 0% -> 0%
where the time goes in v3:
time: 43.8 us; the launch traced here: 43.6 us
  starting transfers between devices  18.1 us (41%)
  matrix products  11.3 us (26%)
  waiting for transfers between devices  8.51 us (19%)
  between operations  2.14 us (5%)
  local copies, waits for them, and re-layouts  2.08 us (5%)
  other arithmetic  1.48 us (3%)
    ppermute x13, starting transfers between devices, exchange(): return lax.ppermute(value, axis, [(i, partner(i)) for i in range(size)])  18.1 us
    dot_general x8, matrix products, local(): jnp.dot(blocks[m], tile_now, precision=high, preferred_element_type=jnp.f...  10 us
    ppermute x13, waiting for transfers between devices, exchange(): return lax.ppermute(value, axis, [(i, partner(i)) for i in range(size)])  8.51 us
    slice x1, local copies, waits for them, and re-layouts, local(): offset = eval_energy[energy] - band_level - frequency_rows  1.33 us
  transfers between devices with their start and end apart: 13, of which 6 were waited for; matrix products, arithmetic and copies ran while one was open for 25% of the time, Pallas kernels for 0%

profile of v3, /device:TPU:0, one launch (start us, length us, event | category | flops | bytes accessed | tf_op | source)
XLA Modules:
  0.0 43.6 jit_solution(4742200054866683262)
XLA Ops:
  0.0 0.7 %broadcast_subtract_fusion = s32[1,512]{1,0:T(1,128)S(1)} fusion(s32[1,512]{1,0:T(1,128)} %param.7, s32[]{:T(128)S(6)} %mul.105), kind=kLoop, calls=%fused_computation.98 | loop fusion | flops 512 | bytes 4100 | tf_op jit(solution)/shard_map/sub | solution.py:39
  1.0 0.7 %fusion.47 = f32[512,128]{1,0:T(8,128)S(1)} fusion(s32[512]{0:T(512)S(1)} %bitcast.26, f32[1,128,512]{2,1,0:T(8,128)S(1)} %copy-done), kind=kOutput, calls=%fused_computation.60 | convolution fusion | flops 403177472 | bytes 526336 | tf_op jit(solution)/shard_map/dot_general | solution.py:14
  2.2 2.6 %collective-permute-start.2 = (f32[128,512]{0,1:T(8,128)S(1)}, f32[128,512]{0,1:T(8,128)S(1)}, u32[]{:S(2)}, u32[]{:S(2)}) collective-permute-start(f32[128,512]{0,1:T(8,128)S(1)} %bitcast.24), channel_id=1, source_target_pairs={{0,3},{1,2},{2,1},{3,0},{4,7},{5,6},{6,5},{7,4},{8,11},{9,10},{10,... | collective-permute-start | bytes 786440 | tf_op jit(solution)/shard_map/ppermute | solution.py:22
  4.9 1.3 %fusion.99 = (f32[1]{0:T(128)}, f32[1]{0:T(128)}) fusion(f32[2]{0:T(128)} %param.9), kind=kLoop, calls=%fused_computation.115 | loop fusion | bytes 16 | tf_op jit(solution)/shard_map/slice | solution.py:64
  7.5 2.2 %fusion.18 = f32[128,512]{1,0:T(8,128)S(1)} fusion(f32[512,128]{1,0:T(8,128)S(1)} %fusion.47, f32[2048,512]{1,0:T(8,128)} %param.11, s32[]{:T(128)S(6)} %select_n.8, f32[2048,512]{1,0:T(8,128)} %param.10, f32[]{:T(128)} %bitcast.2), kind=kOutput, calls=%fused_computation.31 | convolution fusion | flops 203161600 | bytes 2621956 | tf_op jit(solution)/shard_map/dot_general | solution.py:67
  10.4 2.4 %fusion.20 = f32[128,512]{1,0:T(8,128)S(1)} fusion(f32[512,128]{1,0:T(8,128)S(1)} %fusion.47, f32[2048,512]{1,0:T(8,128)} %param.11, s32[]{:T(128)S(6)} %select_n.8, f32[2048,512]{1,0:T(8,128)} %param.10, f32[]{:T(128)} %bitcast.5), kind=kOutput, calls=%fused_computation.33 | convolution fusion | flops 203161600 | bytes 2621956 | tf_op jit(solution)/shard_map/dot_general | solution.py:67
  13.2 2.1 %convolution_add_fusion.3 = f32[128,512]{1,0:T(8,128)S(1)} fusion(f32[128,512]{1,0:T(8,128)S(1)} %fusion.18, f32[128,512]{0,1:T(8,128)S(1)} %collective-permute-done, f32[2048,512]{1,0:T(8,128)S(1)} %copy-done.1, s32[]{:T(128)S(6)} %select_n.9, f32[2048,512]{1,0:T(8,128)} %param.10, f32[]{:T(128)} %bitcast.2), kind=kOutput, calls=%fused_computation.5 | convolution fusion | flops 203227136 | bytes 2884100 | tf_op jit(solution)/shard_map/dot_general | solution.py:67
  16.1 1.2 %collective-permute-done.1 = f32[128,512]{0,1:T(8,128)S(1)} collective-permute-done((f32[128,512]{0,1:T(8,128)S(1)}, f32[128,512]{0,1:T(8,128)S(1)}, u32[]{:S(2)}, u32[]{:S(2)}) %collective-permute-start.1) | collective-permute-done | bytes 262176 | tf_op jit(solution)/shard_map/ppermute | solution.py:22
  17.3 0.7 %fusion.1 = f32[128,512]{1,0:T(8,128)S(1)} fusion(f32[128,512]{1,0:T(8,128)S(1)} %fusion.19, f32[128,512]{1,0:T(8,128)S(1)} %convolution_add_fusion.3, f32[128,512]{0,1:T(8,128)S(1)} %collective-permute-done.1, f32[2048,512]{1,0:T(8,128)S(1)} %copy-done.1, s32[]{:T(128)S(6)} %select_n.10, f32[2048,512]{1,0:T(8,128)S(1)} %copy-done.2, f32[]{:T(128)} %bitcast.2), kind=kOutput, calls=%fused_computation.4 | convolution fusion | flops 203292672 | bytes 3145736 | tf_op jit(solution)/shard_map/dot_general | solution.py:67
  18.4 0.7 %fusion.21 = f32[128,512]{1,0:T(8,128)S(1)} fusion(f32[128,512]{0,1:T(8,128)S(1)} %collective-permute-done.2, f32[2048,512]{1,0:T(8,128)S(1)} %copy-done.1, s32[]{:T(128)S(6)} %select_n.11, f32[2048,512]{1,0:T(8,128)S(1)} %copy-done.2, f32[]{:T(128)} %bitcast.5), kind=kOutput, calls=%fused_computation.34 | convolution fusion | flops 203161600 | bytes 2621448 | tf_op jit(solution)/shard_map/dot_general | solution.py:67
  19.1 0.7 %convolution_add_fusion.1 = f32[128,512]{1,0:T(8,128)S(1)} fusion(f32[128,512]{1,0:T(8,128)S(1)} %fusion.20, f32[128,512]{0,1:T(8,128)S(1)} %collective-permute-done, f32[2048,512]{1,0:T(8,128)S(1)} %copy-done.1, s32[]{:T(128)S(6)} %select_n.9, f32[2048,512]{1,0:T(8,128)S(1)} %copy-done.2, f32[]{:T(128)} %bitcast.5), kind=kOutput, calls=%fused_computation.2 | convolution fusion | flops 203227136 | bytes 2883592 | tf_op jit(solution)/shard_map/dot_general | solution.py:67
  19.7 0.7 %fusion = f32[128,512]{1,0:T(8,128)S(1)} fusion(f32[128,512]{1,0:T(8,128)S(1)} %fusion.21, f32[128,512]{1,0:T(8,128)S(1)} %convolution_add_fusion.1, f32[128,512]{0,1:T(8,128)S(1)} %collective-permute-done.1, f32[2048,512]{1,0:T(8,128)S(1)} %copy-done.1, s32[]{:T(128)S(6)} %select_n.10, f32[2048,512]{1,0:T(8,128)S(1)} %copy-done.2, f32[]{:T(128)} %bitcast.5), kind=kOutput, calls=%fused_computation.1 | convolution fusion | flops 203292672 | bytes 3145736 | tf_op jit(solution)/shard_map/dot_general | solution.py:67
  21.3 1.8 %collective-permute-start.4 = (f32[128,128]{1,0:T(8,128)S(1)}, f32[128,128]{1,0:T(8,128)S(1)}, u32[]{:S(2)}, u32[]{:S(2)}) collective-permute-start(f32[128,128]{1,0:T(8,128)S(1)} %add.107), channel_id=1, source_target_pairs={{0,2},{1,3},{2,0},{3,1},{4,6},{5,7},{6,4},{7,5},{8,10},{9,11},{10,... | collective-permute-start | bytes 196616 | tf_op jit(solution)/shard_map/ppermute | solution.py:22
  23.0 0.9 %collective-permute-start.9 = (f32[128,128]{1,0:T(8,128)S(1)}, f32[128,128]{1,0:T(8,128)S(1)}, u32[]{:S(2)}, u32[]{:S(2)}) collective-permute-start(f32[128,128]{1,0:T(8,128)S(1)} %add.119), channel_id=1, source_target_pairs={{0,2},{1,3},{2,0},{3,1},{4,6},{5,7},{6,4},{7,5},{8,10},{9,11},{10,... | collective-permute-start | bytes 196616 | tf_op jit(solution)/shard_map/ppermute | solution.py:22
  23.9 1.8 %collective-permute-done.4 = f32[128,128]{1,0:T(8,128)S(1)} collective-permute-done((f32[128,128]{1,0:T(8,128)S(1)}, f32[128,128]{1,0:T(8,128)S(1)}, u32[]{:S(2)}, u32[]{:S(2)}) %collective-permute-start.4) | collective-permute-done | bytes 65568 | tf_op jit(solution)/shard_map/ppermute | solution.py:22
  25.7 1.9 %collective-permute-start.5 = (f32[128,128]{1,0:T(8,128)S(1)}, f32[128,128]{1,0:T(8,128)S(1)}, u32[]{:S(2)}, u32[]{:S(2)}) collective-permute-start(f32[128,128]{1,0:T(8,128)S(1)} %add.108), channel_id=1, source_target_pairs={{0,4},{1,5},{2,6},{3,7},{4,0},{5,1},{6,2},{7,3},{8,12},{9,13},{10,... | collective-permute-start | bytes 196616 | tf_op jit(solution)/shard_map/ppermute | solution.py:22
  27.7 1.2 %collective-permute-start.10 = (f32[128,128]{1,0:T(8,128)S(1)}, f32[128,128]{1,0:T(8,128)S(1)}, u32[]{:S(2)}, u32[]{:S(2)}) collective-permute-start(f32[128,128]{1,0:T(8,128)S(1)} %add.120), channel_id=1, source_target_pairs={{0,4},{1,5},{2,6},{3,7},{4,0},{5,1},{6,2},{7,3},{8,12},{9,13},{10,... | collective-permute-start | bytes 196616 | tf_op jit(solution)/shard_map/ppermute | solution.py:22
  28.9 1.2 %collective-permute-done.5 = f32[128,128]{1,0:T(8,128)S(1)} collective-permute-done((f32[128,128]{1,0:T(8,128)S(1)}, f32[128,128]{1,0:T(8,128)S(1)}, u32[]{:S(2)}, u32[]{:S(2)}) %collective-permute-start.5) | collective-permute-done | bytes 65568 | tf_op jit(solution)/shard_map/ppermute | solution.py:22
  30.2 1.9 %collective-permute-start.6 = (f32[128,128]{1,0:T(8,128)S(1)}, f32[128,128]{1,0:T(8,128)S(1)}, u32[]{:S(2)}, u32[]{:S(2)}) collective-permute-start(f32[128,128]{1,0:T(8,128)S(1)} %add.109), channel_id=1, source_target_pairs={{0,8},{1,9},{2,10},{3,11},{4,12},{5,13},{6,14},{7,15},{8,0},{9,1},... | collective-permute-start | bytes 196616 | tf_op jit(solution)/shard_map/ppermute | solution.py:22
  32.1 1.5 %collective-permute-start.11 = (f32[128,128]{1,0:T(8,128)S(1)}, f32[128,128]{1,0:T(8,128)S(1)}, u32[]{:S(2)}, u32[]{:S(2)}) collective-permute-start(f32[128,128]{1,0:T(8,128)S(1)} %add.121), channel_id=1, source_target_pairs={{0,8},{1,9},{2,10},{3,11},{4,12},{5,13},{6,14},{7,15},{8,0},{9,1},... | collective-permute-start | bytes 196616 | tf_op jit(solution)/shard_map/ppermute | solution.py:22
  33.7 0.9 %collective-permute-done.6 = f32[128,128]{1,0:T(8,128)S(1)} collective-permute-done((f32[128,128]{1,0:T(8,128)S(1)}, f32[128,128]{1,0:T(8,128)S(1)}, u32[]{:S(2)}, u32[]{:S(2)}) %collective-permute-start.6) | collective-permute-done | bytes 65568 | tf_op jit(solution)/shard_map/ppermute | solution.py:22
  34.6 3.1 %collective-permute-start.7 = (f32[128,128]{1,0:T(8,128)S(1)}, f32[128,128]{1,0:T(8,128)S(1)}, u32[]{:S(2)}, u32[]{:S(2)}) collective-permute-start(f32[128,128]{1,0:T(8,128)S(1)} %add.110), channel_id=1, source_target_pairs={{0,16},{1,17},{2,18},{3,19},{4,20},{5,21},{6,22},{7,23},{8,24},{9,... | collective-permute-start | bytes 196616 | tf_op jit(solution)/shard_map/ppermute | solution.py:22
  37.7 1.9 %collective-permute-start.12 = (f32[128,128]{1,0:T(8,128)S(1)}, f32[128,128]{1,0:T(8,128)S(1)}, u32[]{:S(2)}, u32[]{:S(2)}) collective-permute-start(f32[128,128]{1,0:T(8,128)S(1)} %add.122), channel_id=1, source_target_pairs={{0,16},{1,17},{2,18},{3,19},{4,20},{5,21},{6,22},{7,23},{8,24},{9,... | collective-permute-start | bytes 196616 | tf_op jit(solution)/shard_map/ppermute | solution.py:22
  39.9 3.0 %collective-permute-done.12 = f32[128,128]{1,0:T(8,128)S(1)} collective-permute-done((f32[128,128]{1,0:T(8,128)S(1)}, f32[128,128]{1,0:T(8,128)S(1)}, u32[]{:S(2)}, u32[]{:S(2)}) %collective-permute-start.12) | collective-permute-done | bytes 65568 | tf_op jit(solution)/shard_map/ppermute | solution.py:22
  (32 shorter events, 4.3 us)
Async XLA Ops:
  0.0 1.0 %copy-start = (f32[1,128,512]{2,1,0:T(8,128)S(1)}, f32[1,128,512]{2,1,0:T(8,128)}, u32[]{:S(2)}) copy-start(f32[1,128,512]{2,1,0:T(8,128)} %param.6) | copy-start | bytes 786436
  1.7 11.1 %collective-permute-start = (f32[128,512]{0,1:T(8,128)S(1)}, f32[128,512]{0,1:T(8,128)S(1)}, u32[]{:S(2)}, u32[]{:S(2)}) collective-permute-start(f32[128,512]{0,1:T(8,128)S(1)} %bitcast.23), channel_id=1, source_target_pairs={{0,1},{1,0},{2,3},{3,2},{4,5},{5,4},{6,7},{7,6},{8,9},{9,8},{10,11... | collective-permute-start | bytes 786440 | tf_op jit(solution)/shard_map/ppermute | solution.py:22
  2.2 13.1 %collective-permute-start.2 = (f32[128,512]{0,1:T(8,128)S(1)}, f32[128,512]{0,1:T(8,128)S(1)}, u32[]{:S(2)}, u32[]{:S(2)}) collective-permute-start(f32[128,512]{0,1:T(8,128)S(1)} %bitcast.24), channel_id=1, source_target_pairs={{0,3},{1,2},{2,1},{3,0},{4,7},{5,6},{6,5},{7,4},{8,11},{9,10},{10,... | collective-permute-start | bytes 786440 | tf_op jit(solution)/shard_map/ppermute | solution.py:22
  4.9 12.5 %collective-permute-start.1 = (f32[128,512]{0,1:T(8,128)S(1)}, f32[128,512]{0,1:T(8,128)S(1)}, u32[]{:S(2)}, u32[]{:S(2)}) collective-permute-start(f32[128,512]{0,1:T(8,128)S(1)} %bitcast.25), channel_id=1, source_target_pairs={{0,2},{1,3},{2,0},{3,1},{4,6},{5,7},{6,4},{7,5},{8,10},{9,11},{10,... | collective-permute-start | bytes 786440 | tf_op jit(solution)/shard_map/ppermute | solution.py:22
  10.4 2.8 %copy-start.1 = (f32[2048,512]{1,0:T(8,128)S(1)}, f32[2048,512]{1,0:T(8,128)}, u32[]{:S(2)}) copy-start(f32[2048,512]{1,0:T(8,128)} %param.11) | copy-start | bytes 12582916
  12.8 2.6 %copy-start.2 = (f32[2048,512]{1,0:T(8,128)S(1)}, f32[2048,512]{1,0:T(8,128)}, u32[]{:S(2)}) copy-start(f32[2048,512]{1,0:T(8,128)} %param.10) | copy-start | bytes 12582916
  18.3 3.0 %collective-permute-start.3 = (f32[128,128]{1,0:T(8,128)S(1)}, f32[128,128]{1,0:T(8,128)S(1)}, u32[]{:S(2)}, u32[]{:S(2)}) collective-permute-start(f32[128,128]{1,0:T(8,128)S(1)} %fusion.100), channel_id=1, source_target_pairs={{0,1},{1,0},{2,3},{3,2},{4,5},{5,4},{6,7},{7,6},{8,9},{9,8},{10,11... | collective-permute-start | bytes 196616 | tf_op jit(solution)/shard_map/ppermute | solution.py:22
  20.7 2.3 %collective-permute-start.8 = (f32[128,128]{1,0:T(8,128)S(1)}, f32[128,128]{1,0:T(8,128)S(1)}, u32[]{:S(2)}, u32[]{:S(2)}) collective-permute-start(f32[128,128]{1,0:T(8,128)S(1)} %fusion.101), channel_id=1, source_target_pairs={{0,1},{1,0},{2,3},{3,2},{4,5},{5,4},{6,7},{7,6},{8,9},{9,8},{10,11... | collective-permute-start | bytes 196616 | tf_op jit(solution)/shard_map/ppermute | solution.py:22
  21.3 4.5 %collective-permute-start.4 = (f32[128,128]{1,0:T(8,128)S(1)}, f32[128,128]{1,0:T(8,128)S(1)}, u32[]{:S(2)}, u32[]{:S(2)}) collective-permute-start(f32[128,128]{1,0:T(8,128)S(1)} %add.107), channel_id=1, source_target_pairs={{0,2},{1,3},{2,0},{3,1},{4,6},{5,7},{6,4},{7,5},{8,10},{9,11},{10,... | collective-permute-start | bytes 196616 | tf_op jit(solution)/shard_map/ppermute | solution.py:22
  23.0 4.6 %collective-permute-start.9 = (f32[128,128]{1,0:T(8,128)S(1)}, f32[128,128]{1,0:T(8,128)S(1)}, u32[]{:S(2)}, u32[]{:S(2)}) collective-permute-start(f32[128,128]{1,0:T(8,128)S(1)} %add.119), channel_id=1, source_target_pairs={{0,2},{1,3},{2,0},{3,1},{4,6},{5,7},{6,4},{7,5},{8,10},{9,11},{10,... | collective-permute-start | bytes 196616 | tf_op jit(solution)/shard_map/ppermute | solution.py:22
  25.7 4.4 %collective-permute-start.5 = (f32[128,128]{1,0:T(8,128)S(1)}, f32[128,128]{1,0:T(8,128)S(1)}, u32[]{:S(2)}, u32[]{:S(2)}) collective-permute-start(f32[128,128]{1,0:T(8,128)S(1)} %add.108), channel_id=1, source_target_pairs={{0,4},{1,5},{2,6},{3,7},{4,0},{5,1},{6,2},{7,3},{8,12},{9,13},{10,... | collective-permute-start | bytes 196616 | tf_op jit(solution)/shard_map/ppermute | solution.py:22
  27.7 4.4 %collective-permute-start.10 = (f32[128,128]{1,0:T(8,128)S(1)}, f32[128,128]{1,0:T(8,128)S(1)}, u32[]{:S(2)}, u32[]{:S(2)}) collective-permute-start(f32[128,128]{1,0:T(8,128)S(1)} %add.120), channel_id=1, source_target_pairs={{0,4},{1,5},{2,6},{3,7},{4,0},{5,1},{6,2},{7,3},{8,12},{9,13},{10,... | collective-permute-start | bytes 196616 | tf_op jit(solution)/shard_map/ppermute | solution.py:22
  30.2 4.3 %collective-permute-start.6 = (f32[128,128]{1,0:T(8,128)S(1)}, f32[128,128]{1,0:T(8,128)S(1)}, u32[]{:S(2)}, u32[]{:S(2)}) collective-permute-start(f32[128,128]{1,0:T(8,128)S(1)} %add.109), channel_id=1, source_target_pairs={{0,8},{1,9},{2,10},{3,11},{4,12},{5,13},{6,14},{7,15},{8,0},{9,1},... | collective-permute-start | bytes 196616 | tf_op jit(solution)/shard_map/ppermute | solution.py:22
  32.1 5.6 %collective-permute-start.11 = (f32[128,128]{1,0:T(8,128)S(1)}, f32[128,128]{1,0:T(8,128)S(1)}, u32[]{:S(2)}, u32[]{:S(2)}) collective-permute-start(f32[128,128]{1,0:T(8,128)S(1)} %add.121), channel_id=1, source_target_pairs={{0,8},{1,9},{2,10},{3,11},{4,12},{5,13},{6,14},{7,15},{8,0},{9,1},... | collective-permute-start | bytes 196616 | tf_op jit(solution)/shard_map/ppermute | solution.py:22
  34.6 5.4 %collective-permute-start.7 = (f32[128,128]{1,0:T(8,128)S(1)}, f32[128,128]{1,0:T(8,128)S(1)}, u32[]{:S(2)}, u32[]{:S(2)}) collective-permute-start(f32[128,128]{1,0:T(8,128)S(1)} %add.110), channel_id=1, source_target_pairs={{0,16},{1,17},{2,18},{3,19},{4,20},{5,21},{6,22},{7,23},{8,24},{9,... | collective-permute-start | bytes 196616 | tf_op jit(solution)/shard_map/ppermute | solution.py:22
  37.7 5.2 %collective-permute-start.12 = (f32[128,128]{1,0:T(8,128)S(1)}, f32[128,128]{1,0:T(8,128)S(1)}, u32[]{:S(2)}, u32[]{:S(2)}) collective-permute-start(f32[128,128]{1,0:T(8,128)S(1)} %add.122), channel_id=1, source_target_pairs={{0,16},{1,17},{2,18},{3,19},{4,20},{5,21},{6,22},{7,23},{8,24},{9,... | collective-permute-start | bytes 196616 | tf_op jit(solution)/shard_map/ppermute | solution.py:22

commit v4 on v3

--- a/solution.py
+++ b/solution.py
@@ -40,33 +40,36 @@
         ordered = permute_band(elements[0], local_index[0])
 
         if is_power_of_two(col_size):
-            sources = [(0, column_group)] + [
-                (m, column_group ^ m) for m in range(1, col_size)
+            held = [(0, ordered)]
+            stage = col_size // 2
+            while stage >= 1:
+                stacked = jnp.stack([value for _, value in held])
+                arrived = exchange(stacked, "col", col_size, lambda i, s=stage: i ^ s)
+                held = held + [(mask ^ stage, arrived[k]) for k, (mask, _) in enumerate(held)]
+                stage //= 2
+            sources = [(column_group ^ mask, value) for mask, value in held]
+        else:
+            sources = [(column_group, ordered)] + [
+                ((column_group + col_size - m) % col_size,
+                 exchange(ordered, "col", col_size, lambda i, m=m: (i + m) % col_size))
+                for m in range(1, col_size)
             ]
-            partner = lambda m: (lambda i: i ^ m)
-        else:
-            sources = [(0, column_group)] + [
-                (m, (column_group + col_size - m) % col_size) for m in range(1, col_size)
-            ]
-            partner = lambda m: (lambda i: (i + m) % col_size)
-        blocks = {0: ordered}
-        for m, _ in sources[1:]:
-            blocks[m] = exchange(ordered, "col", col_size, partner(m))
 
         band_level = band_energy[0]
-        sigmas = []
-        for energy in range(energies):
-            mixed = None
-            for m, owner in sources:
-                start = owner * columns
-                strength_rows = lax.dynamic_slice_in_dim(pole_strength, start, columns, axis=0)
-                frequency_rows = lax.dynamic_slice_in_dim(pole_frequency, start, columns, axis=0)
+        mixed = [None] * energies
+        for owner, block in sources:
+            start = owner * columns
+            strength_rows = lax.dynamic_slice_in_dim(pole_strength, start, columns, axis=0)
+            frequency_rows = lax.dynamic_slice_in_dim(pole_frequency, start, columns, axis=0)
+            for energy in range(energies):
                 offset = eval_energy[energy] - band_level - frequency_rows
                 denominator = 2.0 * frequency_rows * (offset * offset + broadening * broadening)
                 tile_now = strength_rows * offset / denominator
-                part = jnp.dot(blocks[m], tile_now, precision=high, preferred_element_type=jnp.float32)
-                mixed = part if mixed is None else mixed + part
-            sigma = jnp.dot(mixed, ordered.T, precision=high, preferred_element_type=jnp.float32)
+                part = jnp.dot(block, tile_now, precision=high, preferred_element_type=jnp.float32)
+                mixed[energy] = part if mixed[energy] is None else mixed[energy] + part
+        sigmas = []
+        for energy in range(energies):
+            sigma = jnp.dot(mixed[energy], ordered.T, precision=high, preferred_element_type=jnp.float32)
             if is_power_of_two(total_size):
                 sigma = butterfly_sum(sigma, ("pool", "col"), total_size)
             else:

time: 43.8 us -> 42.9 us (0.979)
  starting transfers between devices: 18.1 us -> 15.1 us
  waiting for transfers between devices: 8.51 us -> 10.7 us
    ppermute x13 -> x12, starting transfers between devices: 18.1 us -> 15.1 us  [exchange(): return lax.ppermute(value, axis, [(i, partner(i)) for i in range(size)])]
    ppermute x13 -> x12, waiting for transfers between devices: 8.51 us -> 10.7 us  [exchange(): return lax.ppermute(value, axis, [(i, partner(i)) for i in range(size)])]
  transfers between devices with their start and end apart: 13 -> 12, of which waited for: 6 -> 6; matrix products, arithmetic and copies ran while one was open for 25% -> 24% of each run, Pallas kernels for 0% -> 0%
where the time goes in v4:
time: 42.9 us; the launch traced here: 42.7 us
  starting transfers between devices  15.1 us (35%)
  matrix products  11.3 us (26%)
  waiting for transfers between devices  10.7 us (25%)
  between operations  2.13 us (5%)
  local copies, waits for them, and re-layouts  2 us (5%)
  other arithmetic  1.52 us (4%)
    ppermute x12, starting transfers between devices, exchange(): return lax.ppermute(value, axis, [(i, partner(i)) for i in range(size)])  15.1 us
    ppermute x12, waiting for transfers between devices, exchange(): return lax.ppermute(value, axis, [(i, partner(i)) for i in range(size)])  10.7 us
    dot_general x8, matrix products, local(): jnp.dot(block, tile_now, precision=high, preferred_element_type=jnp.float32)  10.1 us
    slice x1, local copies, waits for them, and re-layouts, local(): offset = eval_energy[energy] - band_level - frequency_rows  1.37 us
  transfers between devices with their start and end apart: 12, of which 6 were waited for; matrix products, arithmetic and copies ran while one was open for 24% of the time, Pallas kernels for 0%

profile of v4, /device:TPU:0, one launch (start us, length us, event | category | flops | bytes accessed | tf_op | source)
XLA Modules:
  0.0 42.7 jit_solution(4757347994820597259)
XLA Ops:
  0.0 0.7 %broadcast_subtract_fusion = s32[1,512]{1,0:T(1,128)S(1)} fusion(s32[1,512]{1,0:T(1,128)} %param.7, s32[]{:T(128)S(6)} %mul.101), kind=kLoop, calls=%fused_computation.103 | loop fusion | flops 512 | bytes 4100 | tf_op jit(solution)/shard_map/sub | solution.py:39
  1.0 0.7 %fusion.47 = f32[512,128]{1,0:T(8,128)S(1)} fusion(s32[512]{0:T(512)S(1)} %bitcast.34, f32[1,128,512]{2,1,0:T(8,128)S(1)} %copy-done), kind=kOutput, calls=%fused_computation.60 | convolution fusion | flops 403177472 | bytes 526336 | tf_op jit(solution)/shard_map/dot_general | solution.py:14
  1.7 3.1 %collective-permute-start = (f32[1,128,512]{1,2,0:T(8,128)S(1)}, f32[1,128,512]{1,2,0:T(8,128)S(1)}, u32[]{:S(2)}, u32[]{:S(2)}) collective-permute-start(f32[1,128,512]{1,2,0:T(8,128)S(1)} %bitcast.32), channel_id=1, source_target_pairs={{0,2},{1,3},{2,0},{3,1},{4,6},{5,7},{6,4},{7,5},{8,10},{9,11},{10,... | collective-permute-start | bytes 786440 | tf_op jit(solution)/shard_map/ppermute | solution.py:22
  4.7 1.4 %fusion.101 = (f32[1]{0:T(128)}, f32[1]{0:T(128)}) fusion(f32[2]{0:T(128)} %param.9), kind=kLoop, calls=%fused_computation.120 | loop fusion | bytes 16 | tf_op jit(solution)/shard_map/slice | solution.py:65
  7.4 2.2 %fusion.20 = f32[128,512]{1,0:T(8,128)S(1)} fusion(f32[512,128]{1,0:T(8,128)S(1)} %fusion.47, f32[2048,512]{1,0:T(8,128)} %param.11, s32[]{:T(128)S(6)} %select_n.16, f32[2048,512]{1,0:T(8,128)} %param.10, f32[]{:T(128)} %bitcast.10), kind=kOutput, calls=%fused_computation.33 | convolution fusion | flops 203161600 | bytes 2621956 | tf_op jit(solution)/shard_map/dot_general | solution.py:68
  10.3 2.4 %fusion.18 = f32[128,512]{1,0:T(8,128)S(1)} fusion(f32[512,128]{1,0:T(8,128)S(1)} %fusion.47, f32[2048,512]{1,0:T(8,128)} %param.11, s32[]{:T(128)S(6)} %select_n.16, f32[2048,512]{1,0:T(8,128)} %param.10, f32[]{:T(128)} %bitcast.2), kind=kOutput, calls=%fused_computation.31 | convolution fusion | flops 203161600 | bytes 2621956 | tf_op jit(solution)/shard_map/dot_general | solution.py:68
  13.1 2.1 %convolution_add_fusion.1 = f32[128,512]{1,0:T(8,128)S(1)} fusion(f32[128,512]{1,0:T(8,128)S(1)} %fusion.20, f32[2048,512]{1,0:T(8,128)S(1)} %copy-done.1, s32[]{:T(128)S(6)} %select_n.17, f32[2048,512]{1,0:T(8,128)} %param.10, f32[]{:T(128)} %bitcast.10, f32[1,128,512]{1,2,0:T(8,128)S(1)} %collective-permute-done), kind=kOutput, calls=%fused_computation.2 | convolution fusion | flops 203227136 | bytes 2884100 | tf_op jit(solution)/shard_map/dot_general | solution.py:68
  15.3 0.7 %convolution_add_fusion.3 = f32[128,512]{1,0:T(8,128)S(1)} fusion(f32[128,512]{1,0:T(8,128)S(1)} %fusion.18, f32[2048,512]{1,0:T(8,128)S(1)} %copy-done.1, s32[]{:T(128)S(6)} %select_n.17, f32[2048,512]{1,0:T(8,128)S(1)} %copy-done.2, f32[]{:T(128)} %bitcast.2, f32[1,128,512]{1,2,0:T(8,128)S(1)} %collective-permute-done), kind=kOutput, calls=%fused_computation.5 | convolution fusion | flops 203227136 | bytes 2883592 | tf_op jit(solution)/shard_map/dot_general | solution.py:68
  16.0 0.7 %fusion.21 = f32[128,512]{1,0:T(8,128)S(1)} fusion(f32[2048,512]{1,0:T(8,128)S(1)} %copy-done.1, s32[]{:T(128)S(6)} %select_n.19, f32[2048,512]{1,0:T(8,128)S(1)} %copy-done.2, f32[]{:T(128)} %bitcast.10, f32[2,128,512]{1,2,0:T(8,128)S(1)} %collective-permute-done.1), kind=kOutput, calls=%fused_computation.34 | convolution fusion | flops 203161600 | bytes 2621448 | tf_op jit(solution)/shard_map/dot_general | solution.py:68
  16.7 0.7 %fusion = f32[128,512]{1,0:T(8,128)S(1)} fusion(f32[128,512]{1,0:T(8,128)S(1)} %fusion.21, f32[128,512]{1,0:T(8,128)S(1)} %convolution_add_fusion.1, f32[2048,512]{1,0:T(8,128)S(1)} %copy-done.1, s32[]{:T(128)S(6)} %select_n.18, f32[2048,512]{1,0:T(8,128)S(1)} %copy-done.2, f32[]{:T(128)} %bitcast.10, f32[2,128,512]{1,2,0:T(8,128)S(1)} %collective-permute-done.1), kind=kOutput, calls=%fused_computation.1 | convolution fusion | flops 203292672 | bytes 3145736 | tf_op jit(solution)/shard_map/dot_general | solution.py:68
  17.7 0.7 %fusion.19 = f32[128,512]{1,0:T(8,128)S(1)} fusion(f32[2048,512]{1,0:T(8,128)S(1)} %copy-done.1, s32[]{:T(128)S(6)} %select_n.19, f32[2048,512]{1,0:T(8,128)S(1)} %copy-done.2, f32[]{:T(128)} %bitcast.2, f32[2,128,512]{1,2,0:T(8,128)S(1)} %collective-permute-done.1), kind=kOutput, calls=%fused_computation.32 | convolution fusion | flops 203161600 | bytes 2621448 | tf_op jit(solution)/shard_map/dot_general | solution.py:68
  18.4 0.7 %fusion.1 = f32[128,512]{1,0:T(8,128)S(1)} fusion(f32[128,512]{1,0:T(8,128)S(1)} %fusion.19, f32[128,512]{1,0:T(8,128)S(1)} %convolution_add_fusion.3, f32[2048,512]{1,0:T(8,128)S(1)} %copy-done.1, s32[]{:T(128)S(6)} %select_n.18, f32[2048,512]{1,0:T(8,128)S(1)} %copy-done.2, f32[]{:T(128)} %bitcast.2, f32[2,128,512]{1,2,0:T(8,128)S(1)} %collective-permute-done.1), kind=kOutput, calls=%fused_computation.4 | convolution fusion | flops 203292672 | bytes 3145736 | tf_op jit(solution)/shard_map/dot_general | solution.py:68
  20.0 0.8 %collective-permute-done.2 = f32[128,128]{1,0:T(8,128)S(1)} collective-permute-done((f32[128,128]{1,0:T(8,128)S(1)}, f32[128,128]{1,0:T(8,128)S(1)}, u32[]{:S(2)}, u32[]{:S(2)}) %collective-permute-start.2) | collective-permute-done | bytes 65568 | tf_op jit(solution)/shard_map/ppermute | solution.py:22
  20.8 1.3 %collective-permute-start.3 = (f32[128,128]{1,0:T(8,128)S(1)}, f32[128,128]{1,0:T(8,128)S(1)}, u32[]{:S(2)}, u32[]{:S(2)}) collective-permute-start(f32[128,128]{1,0:T(8,128)S(1)} %add.99), channel_id=1, source_target_pairs={{0,2},{1,3},{2,0},{3,1},{4,6},{5,7},{6,4},{7,5},{8,10},{9,11},{10,... | collective-permute-start | bytes 196616 | tf_op jit(solution)/shard_map/ppermute | solution.py:22
  22.1 2.6 %collective-permute-done.8 = f32[128,128]{1,0:T(8,128)S(1)} collective-permute-done((f32[128,128]{1,0:T(8,128)S(1)}, f32[128,128]{1,0:T(8,128)S(1)}, u32[]{:S(2)}, u32[]{:S(2)}) %collective-permute-start.8) | collective-permute-done | bytes 65568 | tf_op jit(solution)/shard_map/ppermute | solution.py:22
  24.7 1.6 %collective-permute-start.9 = (f32[128,128]{1,0:T(8,128)S(1)}, f32[128,128]{1,0:T(8,128)S(1)}, u32[]{:S(2)}, u32[]{:S(2)}) collective-permute-start(f32[128,128]{1,0:T(8,128)S(1)} %add.112), channel_id=1, source_target_pairs={{0,4},{1,5},{2,6},{3,7},{4,0},{5,1},{6,2},{7,3},{8,12},{9,13},{10,... | collective-permute-start | bytes 196616 | tf_op jit(solution)/shard_map/ppermute | solution.py:22
  26.2 1.0 %collective-permute-start.4 = (f32[128,128]{1,0:T(8,128)S(1)}, f32[128,128]{1,0:T(8,128)S(1)}, u32[]{:S(2)}, u32[]{:S(2)}) collective-permute-start(f32[128,128]{1,0:T(8,128)S(1)} %add.100), channel_id=1, source_target_pairs={{0,4},{1,5},{2,6},{3,7},{4,0},{5,1},{6,2},{7,3},{8,12},{9,13},{10,... | collective-permute-start | bytes 196616 | tf_op jit(solution)/shard_map/ppermute | solution.py:22
  27.2 2.2 %collective-permute-done.9 = f32[128,128]{1,0:T(8,128)S(1)} collective-permute-done((f32[128,128]{1,0:T(8,128)S(1)}, f32[128,128]{1,0:T(8,128)S(1)}, u32[]{:S(2)}, u32[]{:S(2)}) %collective-permute-start.9) | collective-permute-done | bytes 65568 | tf_op jit(solution)/shard_map/ppermute | solution.py:22
  29.4 1.6 %collective-permute-start.10 = (f32[128,128]{1,0:T(8,128)S(1)}, f32[128,128]{1,0:T(8,128)S(1)}, u32[]{:S(2)}, u32[]{:S(2)}) collective-permute-start(f32[128,128]{1,0:T(8,128)S(1)} %add.113), channel_id=1, source_target_pairs={{0,8},{1,9},{2,10},{3,11},{4,12},{5,13},{6,14},{7,15},{8,0},{9,1},... | collective-permute-start | bytes 196616 | tf_op jit(solution)/shard_map/ppermute | solution.py:22
  31.1 1.1 %collective-permute-start.5 = (f32[128,128]{1,0:T(8,128)S(1)}, f32[128,128]{1,0:T(8,128)S(1)}, u32[]{:S(2)}, u32[]{:S(2)}) collective-permute-start(f32[128,128]{1,0:T(8,128)S(1)} %add.101), channel_id=1, source_target_pairs={{0,8},{1,9},{2,10},{3,11},{4,12},{5,13},{6,14},{7,15},{8,0},{9,1},... | collective-permute-start | bytes 196616 | tf_op jit(solution)/shard_map/ppermute | solution.py:22
  32.2 1.5 %collective-permute-done.10 = f32[128,128]{1,0:T(8,128)S(1)} collective-permute-done((f32[128,128]{1,0:T(8,128)S(1)}, f32[128,128]{1,0:T(8,128)S(1)}, u32[]{:S(2)}, u32[]{:S(2)}) %collective-permute-start.10) | collective-permute-done | bytes 65568 | tf_op jit(solution)/shard_map/ppermute | solution.py:22
  33.8 3.0 %collective-permute-start.11 = (f32[128,128]{1,0:T(8,128)S(1)}, f32[128,128]{1,0:T(8,128)S(1)}, u32[]{:S(2)}, u32[]{:S(2)}) collective-permute-start(f32[128,128]{1,0:T(8,128)S(1)} %add.114), channel_id=1, source_target_pairs={{0,16},{1,17},{2,18},{3,19},{4,20},{5,21},{6,22},{7,23},{8,24},{9,... | collective-permute-start | bytes 196616 | tf_op jit(solution)/shard_map/ppermute | solution.py:22
  36.8 1.7 %collective-permute-start.6 = (f32[128,128]{1,0:T(8,128)S(1)}, f32[128,128]{1,0:T(8,128)S(1)}, u32[]{:S(2)}, u32[]{:S(2)}) collective-permute-start(f32[128,128]{1,0:T(8,128)S(1)} %add.102), channel_id=1, source_target_pairs={{0,16},{1,17},{2,18},{3,19},{4,20},{5,21},{6,22},{7,23},{8,24},{9,... | collective-permute-start | bytes 196616 | tf_op jit(solution)/shard_map/ppermute | solution.py:22
  39.0 3.0 %collective-permute-done.6 = f32[128,128]{1,0:T(8,128)S(1)} collective-permute-done((f32[128,128]{1,0:T(8,128)S(1)}, f32[128,128]{1,0:T(8,128)S(1)}, u32[]{:S(2)}, u32[]{:S(2)}) %collective-permute-start.6) | collective-permute-done | bytes 65568 | tf_op jit(solution)/shard_map/ppermute | solution.py:22
  (31 shorter events, 3.3 us)
Async XLA Ops:
  0.0 1.0 %copy-start = (f32[1,128,512]{2,1,0:T(8,128)S(1)}, f32[1,128,512]{2,1,0:T(8,128)}, u32[]{:S(2)}) copy-start(f32[1,128,512]{2,1,0:T(8,128)} %param.6) | copy-start | bytes 786436
  1.7 11.0 %collective-permute-start = (f32[1,128,512]{1,2,0:T(8,128)S(1)}, f32[1,128,512]{1,2,0:T(8,128)S(1)}, u32[]{:S(2)}, u32[]{:S(2)}) collective-permute-start(f32[1,128,512]{1,2,0:T(8,128)S(1)} %bitcast.32), channel_id=1, source_target_pairs={{0,2},{1,3},{2,0},{3,1},{4,6},{5,7},{6,4},{7,5},{8,10},{9,11},{10,... | collective-permute-start | bytes 786440 | tf_op jit(solution)/shard_map/ppermute | solution.py:22
  10.3 2.8 %copy-start.1 = (f32[2048,512]{1,0:T(8,128)S(1)}, f32[2048,512]{1,0:T(8,128)}, u32[]{:S(2)}) copy-start(f32[2048,512]{1,0:T(8,128)} %param.11) | copy-start | bytes 12582916
  12.7 2.6 %copy-start.2 = (f32[2048,512]{1,0:T(8,128)S(1)}, f32[2048,512]{1,0:T(8,128)}, u32[]{:S(2)}) copy-start(f32[2048,512]{1,0:T(8,128)} %param.10) | copy-start | bytes 12582916
  12.7 3.2 %collective-permute-start.1 = (f32[2,128,512]{1,2,0:T(8,128)S(1)}, f32[2,128,512]{1,2,0:T(8,128)S(1)}, u32[]{:S(2)}, u32[]{:S(2)}) collective-permute-start(f32[2,128,512]{1,2,0:T(8,128)S(1)} %pad_maximum_fusion), channel_id=1, source_target_pairs={{0,1},{1,0},{2,3},{3,2},{4,5},{5,4},{6,7},{7,6},{8,9},{9,8},{10,11... | collective-permute-start | bytes 1572872 | tf_op jit(solution)/shard_map/ppermute | solution.py:22
  17.6 2.3 %collective-permute-start.7 = (f32[128,128]{1,0:T(8,128)S(1)}, f32[128,128]{1,0:T(8,128)S(1)}, u32[]{:S(2)}, u32[]{:S(2)}) collective-permute-start(f32[128,128]{1,0:T(8,128)S(1)} %fusion.103), channel_id=1, source_target_pairs={{0,1},{1,0},{2,3},{3,2},{4,5},{5,4},{6,7},{7,6},{8,9},{9,8},{10,11... | collective-permute-start | bytes 196616 | tf_op jit(solution)/shard_map/ppermute | solution.py:22
  19.4 1.4 %collective-permute-start.2 = (f32[128,128]{1,0:T(8,128)S(1)}, f32[128,128]{1,0:T(8,128)S(1)}, u32[]{:S(2)}, u32[]{:S(2)}) collective-permute-start(f32[128,128]{1,0:T(8,128)S(1)} %fusion.102), channel_id=1, source_target_pairs={{0,1},{1,0},{2,3},{3,2},{4,5},{5,4},{6,7},{7,6},{8,9},{9,8},{10,11... | collective-permute-start | bytes 196616 | tf_op jit(solution)/shard_map/ppermute | solution.py:22
  19.9 4.7 %collective-permute-start.8 = (f32[128,128]{1,0:T(8,128)S(1)}, f32[128,128]{1,0:T(8,128)S(1)}, u32[]{:S(2)}, u32[]{:S(2)}) collective-permute-start(f32[128,128]{1,0:T(8,128)S(1)} %add.111), channel_id=1, source_target_pairs={{0,2},{1,3},{2,0},{3,1},{4,6},{5,7},{6,4},{7,5},{8,10},{9,11},{10,... | collective-permute-start | bytes 196616 | tf_op jit(solution)/shard_map/ppermute | solution.py:22
  20.8 5.4 %collective-permute-start.3 = (f32[128,128]{1,0:T(8,128)S(1)}, f32[128,128]{1,0:T(8,128)S(1)}, u32[]{:S(2)}, u32[]{:S(2)}) collective-permute-start(f32[128,128]{1,0:T(8,128)S(1)} %add.99), channel_id=1, source_target_pairs={{0,2},{1,3},{2,0},{3,1},{4,6},{5,7},{6,4},{7,5},{8,10},{9,11},{10,... | collective-permute-start | bytes 196616 | tf_op jit(solution)/shard_map/ppermute | solution.py:22
  24.7 4.7 %collective-permute-start.9 = (f32[128,128]{1,0:T(8,128)S(1)}, f32[128,128]{1,0:T(8,128)S(1)}, u32[]{:S(2)}, u32[]{:S(2)}) collective-permute-start(f32[128,128]{1,0:T(8,128)S(1)} %add.112), channel_id=1, source_target_pairs={{0,4},{1,5},{2,6},{3,7},{4,0},{5,1},{6,2},{7,3},{8,12},{9,13},{10,... | collective-permute-start | bytes 196616 | tf_op jit(solution)/shard_map/ppermute | solution.py:22
  26.2 4.8 %collective-permute-start.4 = (f32[128,128]{1,0:T(8,128)S(1)}, f32[128,128]{1,0:T(8,128)S(1)}, u32[]{:S(2)}, u32[]{:S(2)}) collective-permute-start(f32[128,128]{1,0:T(8,128)S(1)} %add.100), channel_id=1, source_target_pairs={{0,4},{1,5},{2,6},{3,7},{4,0},{5,1},{6,2},{7,3},{8,12},{9,13},{10,... | collective-permute-start | bytes 196616 | tf_op jit(solution)/shard_map/ppermute | solution.py:22
  29.4 4.3 %collective-permute-start.10 = (f32[128,128]{1,0:T(8,128)S(1)}, f32[128,128]{1,0:T(8,128)S(1)}, u32[]{:S(2)}, u32[]{:S(2)}) collective-permute-start(f32[128,128]{1,0:T(8,128)S(1)} %add.113), channel_id=1, source_target_pairs={{0,8},{1,9},{2,10},{3,11},{4,12},{5,13},{6,14},{7,15},{8,0},{9,1},... | collective-permute-start | bytes 196616 | tf_op jit(solution)/shard_map/ppermute | solution.py:22
  31.1 5.7 %collective-permute-start.5 = (f32[128,128]{1,0:T(8,128)S(1)}, f32[128,128]{1,0:T(8,128)S(1)}, u32[]{:S(2)}, u32[]{:S(2)}) collective-permute-start(f32[128,128]{1,0:T(8,128)S(1)} %add.101), channel_id=1, source_target_pairs={{0,8},{1,9},{2,10},{3,11},{4,12},{5,13},{6,14},{7,15},{8,0},{9,1},... | collective-permute-start | bytes 196616 | tf_op jit(solution)/shard_map/ppermute | solution.py:22
  33.8 5.2 %collective-permute-start.11 = (f32[128,128]{1,0:T(8,128)S(1)}, f32[128,128]{1,0:T(8,128)S(1)}, u32[]{:S(2)}, u32[]{:S(2)}) collective-permute-start(f32[128,128]{1,0:T(8,128)S(1)} %add.114), channel_id=1, source_target_pairs={{0,16},{1,17},{2,18},{3,19},{4,20},{5,21},{6,22},{7,23},{8,24},{9,... | collective-permute-start | bytes 196616 | tf_op jit(solution)/shard_map/ppermute | solution.py:22
  36.8 5.2 %collective-permute-start.6 = (f32[128,128]{1,0:T(8,128)S(1)}, f32[128,128]{1,0:T(8,128)S(1)}, u32[]{:S(2)}, u32[]{:S(2)}) collective-permute-start(f32[128,128]{1,0:T(8,128)S(1)} %add.102), channel_id=1, source_target_pairs={{0,16},{1,17},{2,18},{3,19},{4,20},{5,21},{6,22},{7,23},{8,24},{9,... | collective-permute-start | bytes 196616 | tf_op jit(solution)/shard_map/ppermute | solution.py:22

commit v5 on v3

--- a/solution.py
+++ b/solution.py
@@ -39,40 +39,49 @@
         local_index = index_map - column_group * columns
         ordered = permute_band(elements[0], local_index[0])
 
-        if is_power_of_two(col_size):
-            sources = [(0, column_group)] + [
-                (m, column_group ^ m) for m in range(1, col_size)
-            ]
-            partner = lambda m: (lambda i: i ^ m)
-        else:
-            sources = [(0, column_group)] + [
-                (m, (column_group + col_size - m) % col_size) for m in range(1, col_size)
-            ]
-            partner = lambda m: (lambda i: (i + m) % col_size)
-        blocks = {0: ordered}
-        for m, _ in sources[1:]:
-            blocks[m] = exchange(ordered, "col", col_size, partner(m))
-
         band_level = band_energy[0]
-        sigmas = []
-        for energy in range(energies):
-            mixed = None
-            for m, owner in sources:
+        states = ordered.shape[0]
+        halves = 2 if states % 16 == 0 else 1
+        rows = states // halves
+        results = []
+        for half in range(halves):
+            own_rows = ordered[half * rows:(half + 1) * rows]
+            if is_power_of_two(col_size):
+                held = [(0, own_rows)]
+                stage = col_size // 2
+                while stage >= 1:
+                    stacked = jnp.stack([value for _, value in held])
+                    arrived = exchange(stacked, "col", col_size, lambda i, s=stage: i ^ s)
+                    held = held + [(mask ^ stage, arrived[k]) for k, (mask, _) in enumerate(held)]
+                    stage //= 2
+                sources = [(column_group ^ mask, value) for mask, value in held]
+            else:
+                sources = [(column_group, own_rows)] + [
+                    ((column_group + col_size - m) % col_size,
+                     exchange(own_rows, "col", col_size, lambda i, m=m: (i + m) % col_size))
+                    for m in range(1, col_size)
+                ]
+            mixed = [None] * energies
+            for owner, block in sources:
                 start = owner * columns
                 strength_rows = lax.dynamic_slice_in_dim(pole_strength, start, columns, axis=0)
                 frequency_rows = lax.dynamic_slice_in_dim(pole_frequency, start, columns, axis=0)
-                offset = eval_energy[energy] - band_level - frequency_rows
-                denominator = 2.0 * frequency_rows * (offset * offset + broadening * broadening)
-                tile_now = strength_rows * offset / denominator
-                part = jnp.dot(blocks[m], tile_now, precision=high, preferred_element_type=jnp.float32)
-                mixed = part if mixed is None else mixed + part
-            sigma = jnp.dot(mixed, ordered.T, precision=high, preferred_element_type=jnp.float32)
+                for energy in range(energies):
+                    offset = eval_energy[energy] - band_level - frequency_rows
+                    denominator = 2.0 * frequency_rows * (offset * offset + broadening * broadening)
+                    tile_now = strength_rows * offset / denominator
+                    part = jnp.dot(block, tile_now, precision=high, preferred_element_type=jnp.float32)
+                    mixed[energy] = part if mixed[energy] is None else mixed[energy] + part
+            sigma = jnp.stack([
+                jnp.dot(mixed[energy], ordered.T, precision=high, preferred_element_type=jnp.float32)
+                for energy in range(energies)
+            ])
             if is_power_of_two(total_size):
                 sigma = butterfly_sum(sigma, ("pool", "col"), total_size)
             else:
                 sigma = lax.psum(sigma, ("pool", "col"))
-            sigmas.append(sigma)
-        return jnp.stack(sigmas)
+            results.append(sigma)
+        return jnp.concatenate(results, axis=1)
 
     return local
 

time: 43.8 us -> 44.4 us (1.014)
  other arithmetic: 1.48 us -> 6 us
  matrix products: 11.3 us -> 8.48 us
  waiting for transfers between devices: 8.51 us -> 6.72 us
  starting transfers between devices: 18.1 us -> 19.5 us
  local copies, waits for them, and re-layouts: 2.08 us -> 1.54 us
    div x0 -> x1, other arithmetic: none -> 4.45 us  [local(): tile_now = strength_rows * offset / denominator]
    dot_general x10 -> x20, matrix products: 10.6 us -> 8 us  [the longest x16 6.93 us: local(): jnp.dot(block, tile_now, precision=high, preferred_element_type=jnp.float32)]
    ppermute x13 -> x14, waiting for transfers between devices: 8.51 us -> 6.72 us  [exchange(): return lax.ppermute(value, axis, [(i, partner(i)) for i in range(size)])]
    ppermute x13 -> x14, starting transfers between devices: 18.1 us -> 19.5 us  [exchange(): return lax.ppermute(value, axis, [(i, partner(i)) for i in range(size)])]
    concatenate x0 -> x1, other arithmetic: none -> 0.67 us  [local(): return jnp.concatenate(results, axis=1)]
    another operation x3 -> x4, other arithmetic: 0.68 us -> 0.05 us  [the longest x2 0.04 us: local(): stacked = jnp.stack([value for _, value in held])]
    unnamed x6 -> x2, local copies, waits for them, and re-layouts: 0.74 us -> 0.24 us
  transfers between devices with their start and end apart: 13 -> 14, of which waited for: 6 -> 5; matrix products, arithmetic and copies ran while one was open for 25% -> 31% of each run, Pallas kernels for 0% -> 0%
where the time goes in v5:
time: 44.4 us; the launch traced here: 44.2 us
  starting transfers between devices  19.5 us (44%)
  matrix products  8.48 us (19%)
  waiting for transfers between devices  6.72 us (15%)
  other arithmetic  6 us (14%)
  between operations  2.03 us (5%)
  local copies, waits for them, and re-layouts  1.54 us (3%)
    ppermute x14, starting transfers between devices, exchange(): return lax.ppermute(value, axis, [(i, partner(i)) for i in range(size)])  19.5 us
    dot_general x16, matrix products, local(): jnp.dot(block, tile_now, precision=high, preferred_element_type=jnp.float32)  6.93 us
    ppermute x14, waiting for transfers between devices, exchange(): return lax.ppermute(value, axis, [(i, partner(i)) for i in range(size)])  6.72 us
    div x1, other arithmetic, local(): tile_now = strength_rows * offset / denominator  4.45 us
    slice x1, local copies, waits for them, and re-layouts, local(): offset = eval_energy[energy] - band_level - frequency_rows  1.28 us
    dot_general x4, matrix products, local(): jnp.dot(mixed[energy], ordered.T, precision=high, preferred_element_type=...  1.08 us
  transfers between devices with their start and end apart: 14, of which 5 were waited for; matrix products, arithmetic and copies ran while one was open for 31% of the time, Pallas kernels for 0%

profile of v5, /device:TPU:0, one launch (start us, length us, event | category | flops | bytes accessed | tf_op | source)
XLA Modules:
  0.0 44.2 jit_solution(8114578228097840825)
XLA Ops:
  0.0 0.7 %broadcast_subtract_fusion = s32[1,512]{1,0:T(1,128)S(1)} fusion(s32[1,512]{1,0:T(1,128)} %param.7, s32[]{:T(128)S(6)} %mul.64), kind=kLoop, calls=%fused_computation.55 | loop fusion | flops 512 | bytes 4100 | tf_op jit(solution)/shard_map/sub | solution.py:39
  1.0 0.5 %fusion.4 = f32[512,128]{0,1:T(8,128)S(1)} fusion(s32[512]{0:T(512)S(1)} %bitcast.74, f32[1,128,512]{2,1,0:T(8,128)S(1)} %copy-done), kind=kOutput, calls=%fused_computation.25 | convolution fusion | flops 402915328 | bytes 526336 | tf_op jit(solution)/shard_map/dot_general | solution.py:14
  1.5 3.1 %collective-permute-start.7 = (f32[1,64,512]{2,1,0:T(8,128)S(1)}, f32[1,64,512]{2,1,0:T(8,128)S(1)}, u32[]{:S(2)}, u32[]{:S(2)}) collective-permute-start(f32[1,64,512]{2,1,0:T(8,128)S(1)} %get-tuple-element.14), channel_id=1, source_target_pairs={{0,2},{1,3},{2,0},{3,1},{4,6},{5,7},{6,4},{7,5},{8,10},{9,11},{10,... | collective-permute-start | bytes 393224 | tf_op jit(solution)/shard_map/ppermute | solution.py:22
  4.6 1.3 %fusion.25 = (f32[1]{0:T(128)}, f32[1]{0:T(128)}) fusion(f32[2]{0:T(128)} %param.9), kind=kLoop, calls=%fused_computation.58 | loop fusion | bytes 16 | tf_op jit(solution)/shard_map/slice | solution.py:70
  7.8 4.5 %multiply_divide_fusion.5 = (f32[512,512]{1,0:T(8,128)S(1)}, f32[512,512]{1,0:T(8,128)S(1)}, f32[512,512]{1,0:T(8,128)S(1)}, f32[512,512]{1,0:T(8,128)S(1)}, f32...) fusion(f32[2048,512]{1,0:T(8,128)} %param.11, ...), kind=kLoop, calls=%fused_computation.21 | loop fusion | flops 13631488 | bytes 16777240 | tf_op jit(solution)/shard_map/div | solution.py:72
  14.1 0.5 %collective-permute-start.1 = (f32[2,64,512]{2,1,0:T(8,128)S(1)}, f32[2,64,512]{2,1,0:T(8,128)S(1)}, u32[]{:S(2)}, u32[]{:S(2)}) collective-permute-start(f32[2,64,512]{2,1,0:T(8,128)S(1)} %pad_maximum_fusion), channel_id=1, source_target_pairs={{0,1},{1,0},{2,3},{3,2},{4,5},{5,4},{6,7},{7,6},{8,9},{9,8},{10,11... | collective-permute-start | bytes 786440 | tf_op jit(solution)/shard_map/ppermute | solution.py:22
  16.4 0.4 fusion.13
  17.7 0.4 %fusion.2 = f32[64,512]{1,0:T(8,128)S(1)} fusion(f32[64,512]{1,0:T(8,128)S(1)} %fusion.14, f32[64,512]{1,0:T(8,128)S(1)} %convolution_add_fusion.3, f32[512,512]{1,0:T(8,128)S(1)} %get-tuple-element.5, f32[2,64,512]{2,1,0:T(8,128)S(1)} %collective-permute-done.8), kind=kOutput, calls=%fused_computation.10 | convolution fusion | flops 100728832 | bytes 1572864 | tf_op jit(solution)/shard_map/dot_general | solution.py:73
  18.8 0.4 fusion.11
  19.9 0.4 fusion.12
  21.1 0.6 %collective-permute-start.2 = (f32[2,64,128]{2,1,0:T(8,128)S(1)}, f32[2,64,128]{2,1,0:T(8,128)S(1)}, u32[]{:S(2)}, u32[]{:S(2)}) collective-permute-start(f32[2,64,128]{2,1,0:T(8,128)S(1)} %pad_maximum_fusion.3), channel_id=1, source_target_pairs={{0,1},{1,0},{2,3},{3,2},{4,5},{5,4},{6,7},{7,6},{8,9},{9,8},{10,11... | collective-permute-start | bytes 196616 | tf_op jit(solution)/shard_map/ppermute | solution.py:22
  21.7 2.0 %collective-permute-start.10 = (f32[2,64,128]{2,1,0:T(8,128)S(1)}, f32[2,64,128]{2,1,0:T(8,128)S(1)}, u32[]{:S(2)}, u32[]{:S(2)}) collective-permute-start(f32[2,64,128]{2,1,0:T(8,128)S(1)} %fusion.23), channel_id=1, source_target_pairs={{0,2},{1,3},{2,0},{3,1},{4,6},{5,7},{6,4},{7,5},{8,10},{9,11},{10,... | collective-permute-start | bytes 196616 | tf_op jit(solution)/shard_map/ppermute | solution.py:22
  23.7 0.9 %collective-permute-start.3 = (f32[2,64,128]{2,1,0:T(8,128)S(1)}, f32[2,64,128]{2,1,0:T(8,128)S(1)}, u32[]{:S(2)}, u32[]{:S(2)}) collective-permute-start(f32[2,64,128]{2,1,0:T(8,128)S(1)} %fusion.24), channel_id=1, source_target_pairs={{0,2},{1,3},{2,0},{3,1},{4,6},{5,7},{6,4},{7,5},{8,10},{9,11},{10,... | collective-permute-start | bytes 196616 | tf_op jit(solution)/shard_map/ppermute | solution.py:22
  24.6 1.4 %collective-permute-done.10 = f32[2,64,128]{2,1,0:T(8,128)S(1)} collective-permute-done((f32[2,64,128]{2,1,0:T(8,128)S(1)}, f32[2,64,128]{2,1,0:T(8,128)S(1)}, u32[]{:S(2)}, u32[]{:S(2)}) %collective-permute-start.10) | collective-permute-done | bytes 65568 | tf_op jit(solution)/shard_map/ppermute | solution.py:22
  26.0 2.3 %collective-permute-start.11 = (f32[2,64,128]{2,1,0:T(8,128)S(1)}, f32[2,64,128]{2,1,0:T(8,128)S(1)}, u32[]{:S(2)}, u32[]{:S(2)}) collective-permute-start(f32[2,64,128]{2,1,0:T(8,128)S(1)} %fusion.51), channel_id=1, source_target_pairs={{0,4},{1,5},{2,6},{3,7},{4,0},{5,1},{6,2},{7,3},{8,12},{9,13},{10,... | collective-permute-start | bytes 196616 | tf_op jit(solution)/shard_map/ppermute | solution.py:22
  28.3 1.3 %collective-permute-start.4 = (f32[2,64,128]{2,1,0:T(8,128)S(1)}, f32[2,64,128]{2,1,0:T(8,128)S(1)}, u32[]{:S(2)}, u32[]{:S(2)}) collective-permute-start(f32[2,64,128]{2,1,0:T(8,128)S(1)} %fusion.50), channel_id=1, source_target_pairs={{0,4},{1,5},{2,6},{3,7},{4,0},{5,1},{6,2},{7,3},{8,12},{9,13},{10,... | collective-permute-start | bytes 196616 | tf_op jit(solution)/shard_map/ppermute | solution.py:22
  29.6 1.2 %collective-permute-done.11 = f32[2,64,128]{2,1,0:T(8,128)S(1)} collective-permute-done((f32[2,64,128]{2,1,0:T(8,128)S(1)}, f32[2,64,128]{2,1,0:T(8,128)S(1)}, u32[]{:S(2)}, u32[]{:S(2)}) %collective-permute-start.11) | collective-permute-done | bytes 65568 | tf_op jit(solution)/shard_map/ppermute | solution.py:22
  30.8 1.9 %collective-permute-start.12 = (f32[2,64,128]{2,1,0:T(8,128)S(1)}, f32[2,64,128]{2,1,0:T(8,128)S(1)}, u32[]{:S(2)}, u32[]{:S(2)}) collective-permute-start(f32[2,64,128]{2,1,0:T(8,128)S(1)} %add.153), channel_id=1, source_target_pairs={{0,8},{1,9},{2,10},{3,11},{4,12},{5,13},{6,14},{7,15},{8,0},{9,1},... | collective-permute-start | bytes 196616 | tf_op jit(solution)/shard_map/ppermute | solution.py:22
  32.7 1.6 %collective-permute-start.5 = (f32[2,64,128]{2,1,0:T(8,128)S(1)}, f32[2,64,128]{2,1,0:T(8,128)S(1)}, u32[]{:S(2)}, u32[]{:S(2)}) collective-permute-start(f32[2,64,128]{2,1,0:T(8,128)S(1)} %add.142), channel_id=1, source_target_pairs={{0,8},{1,9},{2,10},{3,11},{4,12},{5,13},{6,14},{7,15},{8,0},{9,1},... | collective-permute-start | bytes 196616 | tf_op jit(solution)/shard_map/ppermute | solution.py:22
  34.3 0.8 %collective-permute-done.12 = f32[2,64,128]{2,1,0:T(8,128)S(1)} collective-permute-done((f32[2,64,128]{2,1,0:T(8,128)S(1)}, f32[2,64,128]{2,1,0:T(8,128)S(1)}, u32[]{:S(2)}, u32[]{:S(2)}) %collective-permute-start.12) | collective-permute-done | bytes 65568 | tf_op jit(solution)/shard_map/ppermute | solution.py:22
  35.1 3.2 %collective-permute-start.13 = (f32[2,64,128]{2,1,0:T(8,128)S(1)}, f32[2,64,128]{2,1,0:T(8,128)S(1)}, u32[]{:S(2)}, u32[]{:S(2)}) collective-permute-start(f32[2,64,128]{2,1,0:T(8,128)S(1)} %add.154), channel_id=1, source_target_pairs={{0,16},{1,17},{2,18},{3,19},{4,20},{5,21},{6,22},{7,23},{8,24},{9,... | collective-permute-start | bytes 196616 | tf_op jit(solution)/shard_map/ppermute | solution.py:22
  38.3 1.9 %collective-permute-start.6 = (f32[2,64,128]{2,1,0:T(8,128)S(1)}, f32[2,64,128]{2,1,0:T(8,128)S(1)}, u32[]{:S(2)}, u32[]{:S(2)}) collective-permute-start(f32[2,64,128]{2,1,0:T(8,128)S(1)} %add.143), channel_id=1, source_target_pairs={{0,16},{1,17},{2,18},{3,19},{4,20},{5,21},{6,22},{7,23},{8,24},{9,... | collective-permute-start | bytes 196616 | tf_op jit(solution)/shard_map/ppermute | solution.py:22
  40.6 3.0 %collective-permute-done.6 = f32[2,64,128]{2,1,0:T(8,128)S(1)} collective-permute-done((f32[2,64,128]{2,1,0:T(8,128)S(1)}, f32[2,64,128]{2,1,0:T(8,128)S(1)}, u32[]{:S(2)}, u32[]{:S(2)}) %collective-permute-start.6) | collective-permute-done | bytes 65568 | tf_op jit(solution)/shard_map/ppermute | solution.py:22
  43.6 0.7 %pad_maximum_fusion.2 = f32[2,128,128]{2,1,0:T(8,128)} fusion(f32[2,64,128]{2,1,0:T(8,128)S(1)} %add.155, f32[2,64,128]{2,1,0:T(8,128)S(1)} %add.144), kind=kLoop, calls=%fused_computation.34 | loop fusion | flops 32768 | bytes 262144 | tf_op jit(solution)/shard_map/concatenate | solution.py:84
  (46 shorter events, 7.2 us)
Async XLA Ops:
  0.0 1.0 %copy-start = (f32[1,128,512]{2,1,0:T(8,128)S(1)}, f32[1,128,512]{2,1,0:T(8,128)}, u32[]{:S(2)}) copy-start(f32[1,128,512]{2,1,0:T(8,128)} %param.6) | copy-start | bytes 786436
  1.5 12.5 %collective-permute-start.7 = (f32[1,64,512]{2,1,0:T(8,128)S(1)}, f32[1,64,512]{2,1,0:T(8,128)S(1)}, u32[]{:S(2)}, u32[]{:S(2)}) collective-permute-start(f32[1,64,512]{2,1,0:T(8,128)S(1)} %get-tuple-element.14), channel_id=1, source_target_pairs={{0,2},{1,3},{2,0},{3,1},{4,6},{5,7},{6,4},{7,5},{8,10},{9,11},{10,... | collective-permute-start | bytes 393224 | tf_op jit(solution)/shard_map/ppermute | solution.py:22
  4.5 9.5 %collective-permute-start = (f32[1,64,512]{2,1,0:T(8,128)S(1)}, f32[1,64,512]{2,1,0:T(8,128)S(1)}, u32[]{:S(2)}, u32[]{:S(2)}) collective-permute-start(f32[1,64,512]{2,1,0:T(8,128)S(1)} %get-tuple-element.13), channel_id=1, source_target_pairs={{0,2},{1,3},{2,0},{3,1},{4,6},{5,7},{6,4},{7,5},{8,10},{9,11},{10,... | collective-permute-start | bytes 393224 | tf_op jit(solution)/shard_map/ppermute | solution.py:22
  14.0 2.4 %collective-permute-start.8 = (f32[2,64,512]{2,1,0:T(8,128)S(1)}, f32[2,64,512]{2,1,0:T(8,128)S(1)}, u32[]{:S(2)}, u32[]{:S(2)}) collective-permute-start(f32[2,64,512]{2,1,0:T(8,128)S(1)} %pad_maximum_fusion.1), channel_id=1, source_target_pairs={{0,1},{1,0},{2,3},{3,2},{4,5},{5,4},{6,7},{7,6},{8,9},{9,8},{10,11... | collective-permute-start | bytes 786440 | tf_op jit(solution)/shard_map/ppermute | solution.py:22
  14.1 4.7 %collective-permute-start.1 = (f32[2,64,512]{2,1,0:T(8,128)S(1)}, f32[2,64,512]{2,1,0:T(8,128)S(1)}, u32[]{:S(2)}, u32[]{:S(2)}) collective-permute-start(f32[2,64,512]{2,1,0:T(8,128)S(1)} %pad_maximum_fusion), channel_id=1, source_target_pairs={{0,1},{1,0},{2,3},{3,2},{4,5},{5,4},{6,7},{7,6},{8,9},{9,8},{10,11... | collective-permute-start | bytes 786440 | tf_op jit(solution)/shard_map/ppermute | solution.py:22
  18.7 3.0 %collective-permute-start.9 = (f32[2,64,128]{2,1,0:T(8,128)S(1)}, f32[2,64,128]{2,1,0:T(8,128)S(1)}, u32[]{:S(2)}, u32[]{:S(2)}) collective-permute-start(f32[2,64,128]{2,1,0:T(8,128)S(1)} %pad_maximum_fusion.4), channel_id=1, source_target_pairs={{0,1},{1,0},{2,3},{3,2},{4,5},{5,4},{6,7},{7,6},{8,9},{9,8},{10,11... | collective-permute-start | bytes 196616 | tf_op jit(solution)/shard_map/ppermute | solution.py:22
  21.1 2.6 %collective-permute-start.2 = (f32[2,64,128]{2,1,0:T(8,128)S(1)}, f32[2,64,128]{2,1,0:T(8,128)S(1)}, u32[]{:S(2)}, u32[]{:S(2)}) collective-permute-start(f32[2,64,128]{2,1,0:T(8,128)S(1)} %pad_maximum_fusion.3), channel_id=1, source_target_pairs={{0,1},{1,0},{2,3},{3,2},{4,5},{5,4},{6,7},{7,6},{8,9},{9,8},{10,11... | collective-permute-start | bytes 196616 | tf_op jit(solution)/shard_map/ppermute | solution.py:22
  21.7 4.3 %collective-permute-start.10 = (f32[2,64,128]{2,1,0:T(8,128)S(1)}, f32[2,64,128]{2,1,0:T(8,128)S(1)}, u32[]{:S(2)}, u32[]{:S(2)}) collective-permute-start(f32[2,64,128]{2,1,0:T(8,128)S(1)} %fusion.23), channel_id=1, source_target_pairs={{0,2},{1,3},{2,0},{3,1},{4,6},{5,7},{6,4},{7,5},{8,10},{9,11},{10,... | collective-permute-start | bytes 196616 | tf_op jit(solution)/shard_map/ppermute | solution.py:22
  23.7 4.6 %collective-permute-start.3 = (f32[2,64,128]{2,1,0:T(8,128)S(1)}, f32[2,64,128]{2,1,0:T(8,128)S(1)}, u32[]{:S(2)}, u32[]{:S(2)}) collective-permute-start(f32[2,64,128]{2,1,0:T(8,128)S(1)} %fusion.24), channel_id=1, source_target_pairs={{0,2},{1,3},{2,0},{3,1},{4,6},{5,7},{6,4},{7,5},{8,10},{9,11},{10,... | collective-permute-start | bytes 196616 | tf_op jit(solution)/shard_map/ppermute | solution.py:22
  26.0 4.8 %collective-permute-start.11 = (f32[2,64,128]{2,1,0:T(8,128)S(1)}, f32[2,64,128]{2,1,0:T(8,128)S(1)}, u32[]{:S(2)}, u32[]{:S(2)}) collective-permute-start(f32[2,64,128]{2,1,0:T(8,128)S(1)} %fusion.51), channel_id=1, source_target_pairs={{0,4},{1,5},{2,6},{3,7},{4,0},{5,1},{6,2},{7,3},{8,12},{9,13},{10,... | collective-permute-start | bytes 196616 | tf_op jit(solution)/shard_map/ppermute | solution.py:22
  28.3 4.4 %collective-permute-start.4 = (f32[2,64,128]{2,1,0:T(8,128)S(1)}, f32[2,64,128]{2,1,0:T(8,128)S(1)}, u32[]{:S(2)}, u32[]{:S(2)}) collective-permute-start(f32[2,64,128]{2,1,0:T(8,128)S(1)} %fusion.50), channel_id=1, source_target_pairs={{0,4},{1,5},{2,6},{3,7},{4,0},{5,1},{6,2},{7,3},{8,12},{9,13},{10,... | collective-permute-start | bytes 196616 | tf_op jit(solution)/shard_map/ppermute | solution.py:22
  30.8 4.3 %collective-permute-start.12 = (f32[2,64,128]{2,1,0:T(8,128)S(1)}, f32[2,64,128]{2,1,0:T(8,128)S(1)}, u32[]{:S(2)}, u32[]{:S(2)}) collective-permute-start(f32[2,64,128]{2,1,0:T(8,128)S(1)} %add.153), channel_id=1, source_target_pairs={{0,8},{1,9},{2,10},{3,11},{4,12},{5,13},{6,14},{7,15},{8,0},{9,1},... | collective-permute-start | bytes 196616 | tf_op jit(solution)/shard_map/ppermute | solution.py:22
  32.7 5.6 %collective-permute-start.5 = (f32[2,64,128]{2,1,0:T(8,128)S(1)}, f32[2,64,128]{2,1,0:T(8,128)S(1)}, u32[]{:S(2)}, u32[]{:S(2)}) collective-permute-start(f32[2,64,128]{2,1,0:T(8,128)S(1)} %add.142), channel_id=1, source_target_pairs={{0,8},{1,9},{2,10},{3,11},{4,12},{5,13},{6,14},{7,15},{8,0},{9,1},... | collective-permute-start | bytes 196616 | tf_op jit(solution)/shard_map/ppermute | solution.py:22
  35.1 5.4 %collective-permute-start.13 = (f32[2,64,128]{2,1,0:T(8,128)S(1)}, f32[2,64,128]{2,1,0:T(8,128)S(1)}, u32[]{:S(2)}, u32[]{:S(2)}) collective-permute-start(f32[2,64,128]{2,1,0:T(8,128)S(1)} %add.154), channel_id=1, source_target_pairs={{0,16},{1,17},{2,18},{3,19},{4,20},{5,21},{6,22},{7,23},{8,24},{9,... | collective-permute-start | bytes 196616 | tf_op jit(solution)/shard_map/ppermute | solution.py:22
  38.3 5.2 %collective-permute-start.6 = (f32[2,64,128]{2,1,0:T(8,128)S(1)}, f32[2,64,128]{2,1,0:T(8,128)S(1)}, u32[]{:S(2)}, u32[]{:S(2)}) collective-permute-start(f32[2,64,128]{2,1,0:T(8,128)S(1)} %add.143), channel_id=1, source_target_pairs={{0,16},{1,17},{2,18},{3,19},{4,20},{5,21},{6,22},{7,23},{8,24},{9,... | collective-permute-start | bytes 196616 | tf_op jit(solution)/shard_map/ppermute | solution.py:22
